TPU v7x, 128 devices: a whole 4x4x4 slice. The times are simulated.
128 devices in a mesh: wide: 32 (over y, z, core), narrow: 4 (over x).
Axes of the slice: x: 4, y: 4, z: 4, core: 2. Of those that a mesh axis runs over, the one named last changes fastest.
Arguments:
- sources: bfloat16 [32768, 768], P('wide'), may hold values from -8 to 8
- targets: bfloat16 [262144, 768], P(('wide', 'narrow')), may hold values from -8 to 8
- pair_target: int32 [32, 12], replicated, may hold values from 0 to 255, as said below
- pair_count: int32 [32], replicated, may hold values from 8 to 12
Outputs:
- source_potential: float32 [32768], P('wide')
- target_potential: float32 [262144], P(('wide', 'narrow'))
- mapped: bfloat16 [32768, 768], P('wide')
Inputs may be any that keep to these rules, and one draw needn't show every extreme that they name: `pair_target`: source block s lies in row group w = s. Its slots k < 8 hold w * 8 + k, so every target block is paired with some source block. Its other 4 slots hold distinct target blocks of groups w - 1 and w + 1 (taken modulo the number of groups); slot 8 + m holds a block whose position within its group, divided by 2 and rounded down, equals m modulo (4).
All inputs are finite; a program needn't handle non-finite values.
Results may differ from a plain program's by a relative error of at most 0.0044.
Values may be sent and summed in bfloat16 or wider, within the bound.
No kernel may reach another device: no remote copies, remote signals or barrier semaphores. Data moves between devices by JAX's collectives and lax.ppermute only.
A program may use at most 192 MiB of HBM per device.

v0:
```python
import math

import jax
import jax.numpy as jnp
from jax import lax
from jax.sharding import PartitionSpec as P

BLK = 1024
ITERS = 2


epsilon = 0.25
sentinel = -1e30


def passed_along(block, axis, distance):
    devices = range(lax.axis_size(axis))
    route = [((i - distance) % len(devices), i) for i in devices]
    return lax.ppermute(block, axis, route)


def combined_all(x, axis, combine):
    everything = lax.all_gather(x, axis)
    first = everything[0]

    def hop(k, so_far):
        return combine(so_far, everything[k])

    return lax.fori_loop(1, lax.axis_size(axis), hop, first)


def padded(x, sides, width):
    for axis, dim in sides:
        size, length = (lax.axis_size(axis), x.shape[dim])
        up = [(i, (i + 1) % size) for i in range(size)]
        down = [(j, i) for i, j in up]
        last = lax.slice_in_dim(x, length - width, length, axis=dim)
        first = lax.slice_in_dim(x, 0, width, axis=dim)
        before = lax.ppermute(last, axis, up)
        after = lax.ppermute(first, axis, down)
        x = jnp.concatenate([before, x, after], axis=dim)
    return x


def finish_lse(running_max, running_sum):
    present = running_sum > 0
    return jnp.where(present, running_max + jnp.log(jnp.where(present, running_sum, 1.0)), sentinel)


def send_back(partial_value, offset):
    return passed_along(partial_value, "wide", offset)


def row_potentials(partial_value):
    return combined_all(partial_value, "narrow", jnp.logaddexp)


def shards(sources, targets, pair_target, pair_count):
    feature_count = sources.shape[1]
    src_blocks = sources.shape[0] // BLK
    tgt_blocks = targets.shape[0] // BLK
    wide_count = lax.axis_size("wide")
    narrow_count = lax.axis_size("narrow")
    row_group = lax.axis_index("wide")
    column = lax.axis_index("narrow")
    group_blocks = tgt_blocks * narrow_count
    inv_root = 1.0 / math.sqrt(feature_count)
    inv_eps = 1.0 / epsilon
    log_src = -math.log(wide_count * src_blocks * BLK)
    log_tgt = -math.log(wide_count * narrow_count * tgt_blocks * BLK)
    slot_ids = jnp.arange(pair_target.shape[1], dtype=jnp.int32)
    plan_rows = lax.dynamic_slice_in_dim(pair_target, row_group * src_blocks, src_blocks, 0)
    plan_sizes = lax.dynamic_slice_in_dim(pair_count, row_group * src_blocks, src_blocks, 0)
    near_targets = padded(targets, (("wide", 0),), tgt_blocks * BLK)
    near_blocks = 3 * tgt_blocks
    local_ids = jnp.arange(near_blocks, dtype=jnp.int32)
    owner_group = (row_group + local_ids // tgt_blocks - 1 + wide_count) % wide_count
    global_ids = owner_group * group_blocks + column * tgt_blocks + local_ids % tgt_blocks
    listed = (slot_ids[None, :] < plan_sizes[:, None])[:, :, None] & (
        plan_rows[:, :, None] == global_ids[None, None, :]
    )
    linked = jnp.any(listed, axis=1).reshape(-1).astype(jnp.int32)
    unit_range = jnp.arange(src_blocks * near_blocks, dtype=jnp.int32)
    unit_source = unit_range // near_blocks
    unit_target = unit_range % near_blocks
    candidates = linked.shape[0]
    slot_total = near_targets.shape[0] // BLK
    visit_order = jnp.argsort((1 - linked) * candidates + jnp.arange(candidates, dtype=jnp.int32))
    live_count = jnp.sum(linked)

    def locate(position):
        chosen = visit_order[position]
        return (unit_source[chosen], unit_target[chosen])

    def fill_cache(position, score_cache):
        source_slab, target_slab = locate(position)
        col_block = lax.dynamic_slice_in_dim(near_targets, target_slab * BLK, BLK, 0)
        product = lax.dot_general(
            sources, col_block, (((1,), (1,)), ((), ())), preferred_element_type=jnp.float32
        )
        return lax.dynamic_update_index_in_dim(score_cache, product, position, 0)

    score_cache = lax.fori_loop(
        0, live_count, fill_cache, jnp.zeros((candidates, BLK, BLK), jnp.float32)
    )

    def slot_scores(position, potential):
        source_slab, target_slab = locate(position)
        product = lax.dynamic_index_in_dim(score_cache, position, 0, False)
        target_pot = lax.dynamic_slice_in_dim(potential, target_slab * BLK, BLK, 0)
        return (source_slab, target_slab, (target_pot[None, :] + product * inv_root) * inv_eps)

    def row_pass(potential):

        def row_visit(position, state_pair):
            running_max, running_sum = state_pair
            source_slab, target_slab, scores = slot_scores(position, potential)
            old_max = lax.dynamic_index_in_dim(running_max, source_slab, 0, False)
            old_sum = lax.dynamic_index_in_dim(running_sum, source_slab, 0, False)
            new_max = jnp.maximum(old_max, jnp.max(scores, axis=1))
            new_sum = old_sum * jnp.exp(old_max - new_max) + jnp.sum(
                jnp.exp(scores - new_max[:, None]), axis=1
            )
            return (
                lax.dynamic_update_index_in_dim(running_max, new_max, source_slab, 0),
                lax.dynamic_update_index_in_dim(running_sum, new_sum, source_slab, 0),
            )

        start = (
            jnp.full((src_blocks, BLK), sentinel, jnp.float32),
            jnp.zeros((src_blocks, BLK), jnp.float32),
        )
        running_max, running_sum = lax.fori_loop(0, live_count, row_visit, start)
        return finish_lse(running_max, running_sum).reshape(-1)

    def col_pass(source_pot):

        def col_visit(position, state_pair):
            running_max, running_sum = state_pair
            source_slab, target_slab = locate(position)
            product = lax.dynamic_index_in_dim(score_cache, position, 0, False)
            scores = (source_pot[:, None] + product * inv_root) * inv_eps
            old_max = lax.dynamic_index_in_dim(running_max, target_slab, 0, False)
            old_sum = lax.dynamic_index_in_dim(running_sum, target_slab, 0, False)
            new_max = jnp.maximum(old_max, jnp.max(scores, axis=0))
            new_sum = old_sum * jnp.exp(old_max - new_max) + jnp.sum(
                jnp.exp(scores - new_max[None, :]), axis=0
            )
            return (
                lax.dynamic_update_index_in_dim(running_max, new_max, target_slab, 0),
                lax.dynamic_update_index_in_dim(running_sum, new_sum, target_slab, 0),
            )

        start = (
            jnp.full((slot_total, BLK), sentinel, jnp.float32),
            jnp.zeros((slot_total, BLK), jnp.float32),
        )
        running_max, running_sum = lax.fori_loop(0, live_count, col_visit, start)
        return finish_lse(running_max, running_sum)

    near_pot = jnp.zeros((slot_total * BLK,), jnp.float32)
    for iteration in range(ITERS):
        row_lse = row_potentials(row_pass(near_pot))
        source_pot = epsilon * (log_src - row_lse)
        pieces = col_pass(source_pot)
        pieces = pieces.reshape(3, tgt_blocks * BLK)
        col_lse = jnp.logaddexp(
            pieces[1], jnp.logaddexp(send_back(pieces[2], 1), send_back(pieces[0], -1))
        )
        target_pot = epsilon * (log_tgt - col_lse)
        near_pot = padded(target_pot, (("wide", 0),), tgt_blocks * BLK)
    row_lse = row_potentials(row_pass(near_pot))
    source_pot = epsilon * (log_src - row_lse)

    def accumulate(position, numer):
        source_slab, target_slab, scores = slot_scores(position, near_pot)
        weights = jnp.exp(scores - row_lse[:, None]).astype(jnp.bfloat16)
        col_block = lax.dynamic_slice_in_dim(near_targets, target_slab * BLK, BLK, 0)
        partial_value = jnp.dot(weights, col_block, preferred_element_type=jnp.float32)
        return numer + partial_value

    numer = lax.fori_loop(
        0, live_count, accumulate, jnp.zeros((src_blocks * BLK, feature_count), jnp.float32)
    )
    mapped = lax.psum(numer, "narrow").astype(jnp.bfloat16)
    return (source_pot, target_pot, mapped)


def solution(mesh):
    placed = (P("wide", None), P(("wide", "narrow"), None), P(), P())
    return jax.shard_map(
        shards,
        mesh=mesh,
        in_specs=placed,
        out_specs=(P("wide"), P(("wide", "narrow")), P("wide", None)),
        check_vma=False,
    )
```

profile of v0, /device:TPU:98, one launch (start us, length us, event | category | flops | bytes accessed | tf_op | source)
XLA Modules:
  0.0 414.9 jit_solution(16162667421878432902)
XLA Ops:
  6.4 31.4 %collective-permute-done = bf16[2048,768]{1,0:T(8,128)(2,1)} collective-permute-done((bf16[2048,768]{1,0:T(8,128)(2,1)}, bf16[2048,768]{1,0:T(8,128)(2,1)}, u32[]{:S(2)}, u32[]{:S(2)}) %collective-permute-start) | collective-permute-done | bytes 3145760 | tf_op jit(solution)/shard_map/ppermute | solution.py:39
  47.3 11.5 %broadcast_in_dim.54.clone = f32[6,1024,1024]{2,1,0:T(8,128)} broadcast(f32[]{:T(128)} %constant.396.clone.1), dimensions={} | broadcast | bytes 25165828 | tf_op jit(solution)/shard_map/broadcast_in_dim | solution.py:104
  58.8 59.5 %while.130 = (s32[]{:T(128)}, f32[6,1024,1024]{2,1,0:T(8,128)}, s32[]{:T(128)}, s32[6]{0:T(128)S(1)}, s32[6]{0:T(128)S(1)}, /*index=5*/bf16[6144,768]{1,0:T(8,12...) while((s32[]{:T(128)}, f32[6,1024,1024]{2,1,0:T(8,128)}, ...), condition=%wide.region_4.5_spmd, body=%wide.region_3.4_spmd.sunk | while | flops 1610612736 | bytes 24117512 | solution.py:103
  63.2 5.2 %convolution_bitcast_fusion.2 = f32[1,1024,1024]{1,2,0:T(8,128)} fusion(bf16[1024,768]{1,0:T(8,128)(2,1)S(1)} %get-tuple-element.1428, bf16[6144,768]{1,0:T(8,128)(2,1)} %get-tuple-element.1427, s32[]{:T(128)S(6)} %select_n.376), kind=kOutput, calls=%fused_computation.clone.1 | convolution fusion | flops 1610612736 | bytes 7340036 | tf_op jit(solution)/shard_map/while/body/dot_general | solution.py:98
  68.4 5.3 %copy.59 = f32[1,1024,1024]{2,1,0:T(8,128)} copy(f32[1,1024,1024]{1,2,0:T(8,128)} %convolution_bitcast_fusion.2) | data formatting | bytes 8388608 | tf_op jit(solution)/shard_map/while/body/jit(dynamic_update_index_in_dim)/dynamic_update_slice | solution.py:101
  82.8 5.2 %convolution_bitcast_fusion.2 = f32[1,1024,1024]{1,2,0:T(8,128)} fusion(bf16[1024,768]{1,0:T(8,128)(2,1)S(1)} %get-tuple-element.1428, bf16[6144,768]{1,0:T(8,128)(2,1)} %get-tuple-element.1427, s32[]{:T(128)S(6)} %select_n.376), kind=kOutput, calls=%fused_computation.clone.1 | convolution fusion | flops 1610612736 | bytes 7340036 | tf_op jit(solution)/shard_map/while/body/dot_general | solution.py:98
  88.0 5.3 %copy.59 = f32[1,1024,1024]{2,1,0:T(8,128)} copy(f32[1,1024,1024]{1,2,0:T(8,128)} %convolution_bitcast_fusion.2) | data formatting | bytes 8388608 | tf_op jit(solution)/shard_map/while/body/jit(dynamic_update_index_in_dim)/dynamic_update_slice | solution.py:101
  93.3 4.7 %constant_dynamic-update-slice_fusion.5 = f32[6,1024,1024]{2,1,0:T(8,128)} fusion(f32[6,1024,1024]{2,1,0:T(8,128)} %get-tuple-element.1411, f32[1,1024,1024]{2,1,0:T(8,128)} %copy.59, s32[]{:T(128)S(6)} %select_n.374), kind=kLoop, calls=%fused_computation.2.clone.1 | loop fusion | bytes 8388612 | tf_op jit(solution)/shard_map/while/body/jit(dynamic_update_index_in_dim)/dynamic_update_slice | solution.py:101
  102.5 5.2 %convolution_bitcast_fusion.2 = f32[1,1024,1024]{1,2,0:T(8,128)} fusion(bf16[1024,768]{1,0:T(8,128)(2,1)S(1)} %get-tuple-element.1428, bf16[6144,768]{1,0:T(8,128)(2,1)} %get-tuple-element.1427, s32[]{:T(128)S(6)} %select_n.376), kind=kOutput, calls=%fused_computation.clone.1 | convolution fusion | flops 1610612736 | bytes 7340036 | tf_op jit(solution)/shard_map/while/body/dot_general | solution.py:98
  107.7 5.3 %copy.59 = f32[1,1024,1024]{2,1,0:T(8,128)} copy(f32[1,1024,1024]{1,2,0:T(8,128)} %convolution_bitcast_fusion.2) | data formatting | bytes 8388608 | tf_op jit(solution)/shard_map/while/body/jit(dynamic_update_index_in_dim)/dynamic_update_slice | solution.py:101
  113.0 4.7 %constant_dynamic-update-slice_fusion.5 = f32[6,1024,1024]{2,1,0:T(8,128)} fusion(f32[6,1024,1024]{2,1,0:T(8,128)} %get-tuple-element.1411, f32[1,1024,1024]{2,1,0:T(8,128)} %copy.59, s32[]{:T(128)S(6)} %select_n.374), kind=kLoop, calls=%fused_computation.2.clone.1 | loop fusion | bytes 8388612 | tf_op jit(solution)/shard_map/while/body/jit(dynamic_update_index_in_dim)/dynamic_update_slice | solution.py:101
  118.4 19.5 %while.131 = (s32[]{:T(128)}, f32[1,1024]{1,0:T(1,128)S(1)}, f32[1,1024]{1,0:T(1,128)S(1)}, s32[]{:T(128)}, f32[6,1024,1024]{2,1,0:T(8,128)}, /*index=5*/s32[]{:T(128)}, s32[]{:T(128)}, s32[]{:T(128)}) while((s32[]{:T(128)}, f32[1,1024]{1,0:T(1,128)S(1)}, f32[1,1024]{1,0:T(1,128)S(1)}, s32[]{:T(128)}, f32[6,1024,1024]{2,1,0:T(8,128)}, ...), condition=%wide.region_8.9_spmd, body=%wide.region_5.8_spmd.sunk | while | flops 5245957 | bytes 8437887 | solution.py:133
  137.9 10.8 %all-gather = f32[4,1,1024]{2,1,0:T(1,128)S(1)} all-gather(f32[1,1,1024]{2,1,0:T(1,128)S(1)} %fusion.48), channel_id=1, replica_groups=mesh['wide'=32,'narrow'=4] {'narrow'}, dimensions={0}, use_global_device_ids=true | all-gather | bytes 20480 | tf_op jit(solution)/shard_map/all_gather | solution.py:23
  148.9 36.5 %while.133 = (s32[]{:T(128)}, f32[6,1024]{1,0:T(8,128)S(1)}, f32[6,1024]{1,0:T(8,128)S(1)}, s32[]{:T(128)}, s32[6]{0:T(128)S(1)}, /*index=5*/s32[6]{0:T(128)S(1)...) while((s32[]{:T(128)}, f32[6,1024]{1,0:T(8,128)S(1)}, ...), condition=%wide.region_14.15_spmd, body=%wide.region_11.14_spmd.sunk | while | flops 9439243 | bytes 8458499 | solution.py:158
  192.0 32.4 %while.134 = (s32[]{:T(128)}, f32[1,1024]{1,0:T(1,128)S(1)}, f32[1,1024]{1,0:T(1,128)S(1)}, s32[]{:T(128)}, s32[6]{0:T(128)S(1)}, /*index=5*/s32[6]{0:T(128)S(1)...) while((s32[]{:T(128)}, f32[1,1024]{1,0:T(1,128)S(1)}, ...), condition=%wide.region_18.19_spmd, body=%wide.region_15.18_spmd.sunk | while | flops 9440268 | bytes 8454419 | solution.py:133
  224.4 10.8 %all-gather.1 = f32[4,1,1024]{2,1,0:T(1,128)S(1)} all-gather(f32[1,1,1024]{2,1,0:T(1,128)S(1)} %fusion.49), channel_id=1, replica_groups=mesh['wide'=32,'narrow'=4] {'narrow'}, dimensions={0}, use_global_device_ids=true | all-gather | bytes 20480 | tf_op jit(solution)/shard_map/all_gather | solution.py:23
  235.4 36.5 %while.136 = (s32[]{:T(128)}, f32[6,1024]{1,0:T(8,128)S(1)}, f32[6,1024]{1,0:T(8,128)S(1)}, s32[]{:T(128)}, s32[6]{0:T(128)S(1)}, /*index=5*/s32[6]{0:T(128)S(1)...) while((s32[]{:T(128)}, f32[6,1024]{1,0:T(8,128)S(1)}, ...), condition=%wide.region_24.25_spmd, body=%wide.region_21.24_spmd.sunk | while | flops 9439243 | bytes 8458499 | solution.py:158
  278.5 31.3 %while.137 = (s32[]{:T(128)}, f32[1,1024]{1,0:T(1,128)S(1)}, f32[1,1024]{1,0:T(1,128)S(1)}, s32[]{:T(128)}, s32[6]{0:T(128)S(1)}, /*index=5*/s32[6]{0:T(128)S(1)...) while((s32[]{:T(128)}, f32[1,1024]{1,0:T(1,128)S(1)}, ...), condition=%wide.region_28.29_spmd, body=%wide.region_25.28_spmd.sunk | while | flops 9440268 | bytes 8454419 | solution.py:133
  309.8 11.8 %all-gather.2 = f32[4,1,1024]{2,1,0:T(1,128)S(1)} all-gather(f32[1,1,1024]{2,1,0:T(1,128)S(1)} %fusion.50), channel_id=1, replica_groups=mesh['wide'=32,'narrow'=4] {'narrow'}, dimensions={0}, use_global_device_ids=true | all-gather | bytes 20480 | tf_op jit(solution)/shard_map/all_gather | solution.py:23
  322.6 29.1 %while.139 = (s32[]{:T(128)}, f32[1024,768]{1,0:T(8,128)S(1)}, s32[]{:T(128)}, s32[6]{0:T(128)S(1)}, s32[6]{0:T(128)S(1)}, /*index=5*/f32[6144]{0:T(1024)S(1)}, ...) while((s32[]{:T(128)}, f32[1024,768]{1,0:T(8,128)S(1)}, ...), condition=%wide.region_32.33_spmd, body=%wide.region_31.32_spmd.sunk | while | flops 1616642048 | bytes 12075291 | solution.py:182
  326.9 5.1 %fusion.79 = f32[1024,768]{1,0:T(8,128)S(1)} fusion(f32[1024,768]{1,0:T(8,128)S(1)} %get-tuple-element.1671, f32[6,1024,1024]{2,1,0:T(8,128)} %get-tuple-element.1690, s32[]{:T(128)S(6)} %select_n.396, f32[1024]{0:T(1024)S(1)} %get-tuple-element.1691, f32[1024]{0:T(1024)S(1)} %dynamic_slice.263, bf16[6144,768]{1,0:T(8,128)(2,1)} %get-tuple-element.1692, ...), kind=kOutput, calls=%fused_computation.48.clone.1 | convolution fusion | flops 1616642048 | bytes 12066824 | tf_op jit(solution)/shard_map/while/body/dot_general | solution.py:179
  336.4 5.1 %fusion.79 = f32[1024,768]{1,0:T(8,128)S(1)} fusion(f32[1024,768]{1,0:T(8,128)S(1)} %get-tuple-element.1671, f32[6,1024,1024]{2,1,0:T(8,128)} %get-tuple-element.1690, s32[]{:T(128)S(6)} %select_n.396, f32[1024]{0:T(1024)S(1)} %get-tuple-element.1691, f32[1024]{0:T(1024)S(1)} %dynamic_slice.263, bf16[6144,768]{1,0:T(8,128)(2,1)} %get-tuple-element.1692, ...), kind=kOutput, calls=%fused_computation.48.clone.1 | convolution fusion | flops 1616642048 | bytes 12066824 | tf_op jit(solution)/shard_map/while/body/dot_general | solution.py:179
  345.9 5.1 %fusion.79 = f32[1024,768]{1,0:T(8,128)S(1)} fusion(f32[1024,768]{1,0:T(8,128)S(1)} %get-tuple-element.1671, f32[6,1024,1024]{2,1,0:T(8,128)} %get-tuple-element.1690, s32[]{:T(128)S(6)} %select_n.396, f32[1024]{0:T(1024)S(1)} %get-tuple-element.1691, f32[1024]{0:T(1024)S(1)} %dynamic_slice.263, bf16[6144,768]{1,0:T(8,128)(2,1)} %get-tuple-element.1692, ...), kind=kOutput, calls=%fused_computation.48.clone.1 | convolution fusion | flops 1616642048 | bytes 12066824 | tf_op jit(solution)/shard_map/while/body/dot_general | solution.py:179
  351.6 63.2 %all-reduce.1 = bf16[1024,768]{1,0:T(8,128)(2,1)} all-reduce(f32[1024,768]{1,0:T(8,128)S(1)} %get-tuple-element.674), channel_id=1, replica_groups=mesh['wide'=32,'narrow'=4] {'narrow'}, use_global_device_ids=true, to_apply=%region_33.34 | all-reduce | flops 786432 | bytes 4718592 | tf_op jit(solution)/shard_map/psum | solution.py:185
  (218 shorter events, 147.5 us)
Async XLA Ops:
  0.6 3.1 copy-start
  0.6 40.9 %copy-start.1 = (bf16[2048,768]{1,0:T(8,128)(2,1)S(1)}, bf16[2048,768]{1,0:T(8,128)(2,1)}, u32[]{:S(2)}) copy-start(bf16[2048,768]{1,0:T(8,128)(2,1)} %param.25) | copy-start | bytes 9437188
  0.7 37.1 %collective-permute-start = (bf16[2048,768]{1,0:T(8,128)(2,1)}, bf16[2048,768]{1,0:T(8,128)(2,1)}, u32[]{:S(2)}, u32[]{:S(2)}) collective-permute-start(bf16[2048,768]{1,0:T(8,128)(2,1)} %param.25), channel_id=1, source_target_pairs={{0,4},{4,8},{8,12},{12,16},{16,20},{20,24},{24,28},{28,32},{32,36}... | collective-permute-start | bytes 9437192 | tf_op jit(solution)/shard_map/ppermute | solution.py:39
  0.7 42.8 %collective-permute-start.1 = (bf16[2048,768]{1,0:T(8,128)(2,1)}, bf16[2048,768]{1,0:T(8,128)(2,1)}, u32[]{:S(2)}, u32[]{:S(2)}) collective-permute-start(bf16[2048,768]{1,0:T(8,128)(2,1)} %param.25), channel_id=1, source_target_pairs={{4,0},{8,4},{12,8},{16,12},{20,16},{24,20},{28,24},{32,28},{36,32}... | collective-permute-start | bytes 9437192 | tf_op jit(solution)/shard_map/ppermute | solution.py:40
  47.3 11.5 %copy-start.3 = (bf16[1024,768]{1,0:T(8,128)(2,1)S(1)}, bf16[1024,768]{1,0:T(8,128)(2,1)}, u32[]{:S(2)}) copy-start(bf16[1024,768]{1,0:T(8,128)(2,1)} %param.24) | copy-start | bytes 4718596
  185.5 3.1 collective-permute-start.2
  185.6 3.1 collective-permute-start.3
  188.7 3.1 collective-permute-start.4
  188.8 3.1 collective-permute-start.5
  272.0 3.1 collective-permute-start.6
  272.1 3.1 collective-permute-start.7
  275.2 3.3 copy-start.2
  275.2 3.1 collective-permute-start.8
  276.8 1.6 collective-permute-start.9
where the time goes:
time: 418 us; the launch traced here: 415 us
  blocking collectives  96.6 us (23%)
  other arithmetic  93.6 us (22%)
  local copies, waits for them, and re-layouts  75.8 us (18%)
  loops' own time  70.9 us (17%)
  waiting for transfers between devices  36.8 us (9%)
  matrix products  31 us (7%)
  starting transfers between devices  9.12 us (2%)
    psum x1, blocking collectives, shards(): mapped = lax.psum(numer, 'narrow').astype(jnp.bfloat16)  63.2 us
    ppermute x3, waiting for transfers between devices, padded(): before = lax.ppermute(last, axis, up)  33.9 us
    all_gather x3, blocking collectives, combined_all(): everything = lax.all_gather(x, axis)  33.4 us
    dynamic_update_slice x6, local copies, waits for them, and re-layouts, fill_cache(): return lax.dynamic_update_index_in_dim(score_cache, product, position, 0)  30.2 us
    reduce_sum x9, other arithmetic, row_visit(): jnp.sum(jnp.exp(scores - new_max[:, None]), axis=1)  29.1 us
    another operation x2, loops' own time, col_pass(): running_max, running_sum = lax.fori_loop(0, live_count, col_visit, start)  28.3 us
    reduce_max x9, other arithmetic, row_visit(): new_max = jnp.maximum(old_max, jnp.max(scores, axis=1))  24.6 us
    another operation x3, loops' own time, row_pass(): running_max, running_sum = lax.fori_loop(0, live_count, row_visit, start)  22 us
  transfers between devices with their start and end apart: 10, of which 7 were waited for; matrix products, arithmetic and copies ran while one was open for 2% of the time, Pallas kernels for 0%

commit v1 on v0

v1 whole, which is shorter than its diff:
```python
import math

import jax
import jax.numpy as jnp
from jax import lax
from jax.sharding import PartitionSpec as P

BLK = 1024
ITERS = 2


epsilon = 0.25
sentinel = -1e30


def shifted(x, axis, distance):
    size = lax.axis_size(axis)
    route = [(i, (i + distance) % size) for i in range(size)]
    return lax.ppermute(x, axis, route)


def lse_rows(scores):
    top = jnp.max(scores, axis=1)
    return top + jnp.log(jnp.sum(jnp.exp(scores - top[:, None]), axis=1))


def lse_cols(scores):
    top = jnp.max(scores, axis=0)
    return top + jnp.log(jnp.sum(jnp.exp(scores - top[None, :]), axis=0))


def narrow_lse(partial_value, column, narrow_count):
    pieces = [partial_value] + [shifted(partial_value, "narrow", k) for k in range(1, narrow_count)]
    stacked = jnp.stack(pieces)
    order = (column - jnp.arange(narrow_count, dtype=jnp.int32)) % narrow_count
    ordered = stacked[order]
    top = jnp.max(ordered, axis=0)
    return top + jnp.log(jnp.sum(jnp.exp(ordered - top[None, :]), axis=0))


def shards(sources, targets, pair_target, pair_count):
    feature_count = sources.shape[1]
    tgt_blocks = targets.shape[0] // BLK
    wide_count = lax.axis_size("wide")
    narrow_count = lax.axis_size("narrow")
    w = lax.axis_index("wide")
    c = lax.axis_index("narrow")
    group_blocks = tgt_blocks * narrow_count
    scale = (1.0 / math.sqrt(feature_count)) * (1.0 / epsilon)
    inv_eps = 1.0 / epsilon
    log_src = -math.log(wide_count * sources.shape[0])
    log_tgt = -math.log(wide_count * narrow_count * targets.shape[0])

    left = (w - 1 + wide_count) % wide_count
    right = (w + 1) % wide_count
    slot = group_blocks + c

    mine = pair_target[w, slot]
    mine_live = pair_count[w] > slot
    mine_from_left = (mine // group_blocks) == left

    want_right = pair_target[right, slot]
    want_right_live = (pair_count[right] > slot) & ((want_right // group_blocks) == w)
    want_left = pair_target[left, slot]
    want_left_live = (pair_count[left] > slot) & ((want_left // group_blocks) == w)

    blocks = targets.reshape(tgt_blocks, BLK, feature_count)
    to_right = blocks[want_right % tgt_blocks]
    to_left = blocks[want_left % tgt_blocks]
    from_left = shifted(to_right, "wide", 1)
    from_right = shifted(to_left, "wide", -1)

    own = lax.dot_general(
        sources, targets, (((1,), (1,)), ((), ())), preferred_element_type=jnp.float32
    ) * scale
    extra = jnp.where(mine_from_left, from_left, from_right)
    extra_dots = lax.dot_general(
        sources, extra, (((1,), (1,)), ((), ())), preferred_element_type=jnp.float32
    ) * scale
    z = jnp.concatenate([own, extra_dots], axis=1)

    extra_mask = jnp.where(mine_live, 0.0, sentinel).astype(jnp.float32)

    def row_lse(g_own, g_extra):
        gs = jnp.concatenate([g_own * inv_eps, g_extra * inv_eps + extra_mask])
        return narrow_lse(lse_rows(z + gs[None, :]), c, narrow_count)

    g_own = jnp.zeros((tgt_blocks * BLK,), jnp.float32)
    g_extra = jnp.zeros((BLK,), jnp.float32)
    for iteration in range(ITERS):
        row = row_lse(g_own, g_extra)
        f = epsilon * (log_src - row)
        cols = lse_cols(z + (f * inv_eps)[:, None])
        own_cols = cols[: tgt_blocks * BLK].reshape(tgt_blocks, BLK)
        extra_cols = jnp.where(mine_live, cols[tgt_blocks * BLK:], sentinel)
        back_from_right = shifted(extra_cols, "wide", -1)
        back_from_left = shifted(extra_cols, "wide", 1)
        ids = jnp.arange(tgt_blocks, dtype=jnp.int32)[:, None]
        add_right = jnp.where(want_right_live & (ids == want_right % tgt_blocks), back_from_right[None, :], sentinel)
        add_left = jnp.where(want_left_live & (ids == want_left % tgt_blocks), back_from_left[None, :], sentinel)
        top = jnp.maximum(own_cols, jnp.maximum(add_right, add_left))
        total = jnp.exp(own_cols - top) + jnp.exp(add_right - top) + jnp.exp(add_left - top)
        col = top + jnp.log(total)
        g_blocks = epsilon * (log_tgt - col)
        g_own = g_blocks.reshape(-1)
        send_right = g_blocks[want_right % tgt_blocks]
        send_left = g_blocks[want_left % tgt_blocks]
        g_extra = jnp.where(mine_from_left, shifted(send_right, "wide", 1), shifted(send_left, "wide", -1))

    row = row_lse(g_own, g_extra)
    source_pot = epsilon * (log_src - row)
    gs = jnp.concatenate([g_own * inv_eps, g_extra * inv_eps + extra_mask])
    weights = jnp.exp(z + gs[None, :] - row[:, None]).astype(jnp.bfloat16)
    numer = jnp.dot(weights[:, : tgt_blocks * BLK], targets, preferred_element_type=jnp.float32)
    numer = numer + jnp.dot(weights[:, tgt_blocks * BLK:], extra, preferred_element_type=jnp.float32)

    rows = sources.shape[0]
    part = rows // narrow_count
    mine_part = lax.dynamic_slice_in_dim(numer, c * part, part, 0)
    for k in range(1, narrow_count):
        dest = (c + k) % narrow_count
        piece = lax.dynamic_slice_in_dim(numer, dest * part, part, 0)
        mine_part = mine_part + shifted(piece, "narrow", k)
    done = mine_part.astype(jnp.bfloat16)
    pieces = jnp.stack([done] + [shifted(done, "narrow", k) for k in range(1, narrow_count)])
    order = (c - jnp.arange(narrow_count, dtype=jnp.int32)) % narrow_count
    mapped = pieces[order].reshape(rows, feature_count)
    return (source_pot, g_own, mapped)


def solution(mesh):
    placed = (P("wide", None), P(("wide", "narrow"), None), P(), P())
    return jax.shard_map(
        shards,
        mesh=mesh,
        in_specs=placed,
        out_specs=(P("wide"), P(("wide", "narrow")), P("wide", None)),
        check_vma=False,
    )
```

time: 418 us -> 225 us (0.54)
  the two profiles are of different devices: /device:TPU:98 before, /device:TPU:121 now
where the time goes in v1:
time: 225 us; the launch traced here: 224 us
  waiting for transfers between devices  96.3 us (43%)
  other arithmetic  68.2 us (30%)
  matrix products  19.4 us (9%)
  starting transfers between devices  16.8 us (7%)
  local copies, waits for them, and re-layouts  12.7 us (6%)
  between operations  10.8 us (5%)
    ppermute x25, waiting for transfers between devices, shifted(): return lax.ppermute(x, axis, route)  96.3 us
    reduce_sum x3, other arithmetic, lse_rows(): return top + jnp.log(jnp.sum(jnp.exp(scores - top[:, None]), axis=1))  19 us
    ppermute x25, starting transfers between devices, shifted(): return lax.ppermute(x, axis, route)  16.8 us
    reduce_max x3, other arithmetic, lse_rows(): top = jnp.max(scores, axis=1)  16.7 us
    reduce_max x2, other arithmetic, lse_cols(): top = jnp.max(scores, axis=0)  11.8 us
    reduce_sum x2, other arithmetic, lse_cols(): return top + jnp.log(jnp.sum(jnp.exp(scores - top[None, :]), axis=0))  10.6 us
    dot_general x1, matrix products, shards(): lax.dot_general(sources, targets, (((1,), (1,)), ((), ())), preferred_ele...  7.54 us
    convert_element_type x1, other arithmetic, shards(): weights = jnp.exp(z + gs[None, :] - row[:, None]).astype(jnp.bfloat16)  6.35 us
  transfers between devices with their start and end apart: 25, of which 23 were waited for; matrix products, arithmetic and copies ran while one was open for 4% of the time, Pallas kernels for 0%

profile of v1, /device:TPU:121, one launch (start us, length us, event | category | flops | bytes accessed | tf_op | source)
XLA Modules:
  0.0 224.2 jit_solution(10574374471605478295)
XLA Ops:
  14.9 7.5 %convolution_multiply_fusion = f32[1024,2048]{1,0:T(8,128)} fusion(bf16[1024,768]{1,0:T(8,128)(2,1)S(1)} %copy-done, bf16[2048,768]{1,0:T(8,128)(2,1)} %param.5), kind=kOutput, calls=%fused_computation.16 | convolution fusion | flops 3223322624 | bytes 13107200 | tf_op jit(solution)/shard_map/dot_general | solution.py:73
  22.5 4.5 %collective-permute-done = bf16[1024,768]{1,0:T(8,128)(2,1)} collective-permute-done((bf16[1024,768]{1,0:T(8,128)(2,1)}, bf16[1024,768]{1,0:T(8,128)(2,1)}, u32[]{:S(2)}, u32[]{:S(2)}) %collective-permute-start) | collective-permute-done | bytes 1572896 | tf_op jit(solution)/shard_map/ppermute | solution.py:19
  27.0 5.6 %collective-permute-done.1 = bf16[1024,768]{1,0:T(8,128)(2,1)} collective-permute-done((bf16[1024,768]{1,0:T(8,128)(2,1)S(1)}, bf16[1024,768]{1,0:T(8,128)(2,1)}, u32[]{:S(2)}, u32[]{:S(2)}) %collective-permute-start.1) | collective-permute-done | bytes 1572896 | tf_op jit(solution)/shard_map/ppermute | solution.py:19
  32.6 5.2 %multiply_bitcast_fusion = f32[1024,1024]{1,0:T(8,128)} fusion(bf16[1024,768]{1,0:T(8,128)(2,1)S(1)} %copy-done, bf16[1024,768]{1,0:T(8,128)(2,1)} %collective-permute-done, bf16[1024,768]{1,0:T(8,128)(2,1)} %collective-permute-done.1, pred[]{:T(512)S(6)} %eq.56), kind=kOutput, calls=%fused_computation.19 | convolution fusion | flops 1612447744 | bytes 8912897 | tf_op jit(solution)/shard_map/dot_general | solution.py:77
  37.8 5.6 %add_reduce_fusion.3 = f32[1024]{0:T(1024)S(1)} fusion(f32[3072]{0:T(1024)S(1)} %concatenate.14, f32[1024,1024]{1,0:T(8,128)} %multiply_bitcast_fusion, f32[1024,2048]{1,0:T(8,128)} %convolution_multiply_fusion), kind=kLoop, calls=%fused_computation.14 | loop fusion | flops 9436160 | bytes 12599296 | tf_op jit(solution)/shard_map/reduce_max | solution.py:23
  43.4 6.3 %exponential_reduce_fusion.4 = f32[1024]{0:T(1024)S(1)} fusion(f32[1024]{0:T(1024)S(1)} %add_reduce_fusion.3, f32[3072]{0:T(1024)S(1)} %concatenate.14, f32[1024,1024]{1,0:T(8,128)} %multiply_bitcast_fusion, f32[1024,2048]{1,0:T(8,128)} %convolution_multiply_fusion), kind=kLoop, calls=%fused_computation.10 | loop fusion | flops 12581888 | bytes 12603392 | tf_op jit(solution)/shard_map/reduce_sum | solution.py:24
  57.2 5.9 %add_reduce_fusion.2 = f32[3072]{0:T(1024)S(1)} fusion(f32[1024]{0:T(1024)S(1)} %add_subtract_fusion.2, f32[1024,1024]{1,0:T(8,128)} %multiply_bitcast_fusion, f32[1024,2048]{1,0:T(8,128)} %convolution_multiply_fusion), kind=kLoop, calls=%fused_computation.13 | loop fusion | flops 9434112 | bytes 12599296 | tf_op jit(solution)/shard_map/reduce_max | solution.py:28
  63.1 5.3 %exponential_reduce_fusion.3 = f32[3072]{0:T(1024)S(1)} fusion(f32[3072]{0:T(1024)S(1)} %add_reduce_fusion.2, f32[1024]{0:T(1024)S(1)} %add_subtract_fusion.2, f32[1024,1024]{1,0:T(8,128)S(1)} %copy-done.1, f32[1024,2048]{1,0:T(8,128)} %convolution_multiply_fusion), kind=kLoop, calls=%fused_computation.9 | loop fusion | flops 12579840 | bytes 12611584 | tf_op jit(solution)/shard_map/reduce_sum | solution.py:29
  71.1 5.6 %collective-permute-done.5 = f32[1024]{0:T(1024)S(1)} collective-permute-done((f32[1024]{0:T(1024)S(1)}, f32[1024]{0:T(1024)S(1)}, u32[]{:S(2)}, u32[]{:S(2)}) %collective-permute-start.5) | collective-permute-done | bytes 4128 | tf_op jit(solution)/shard_map/ppermute | solution.py:19
  78.1 5.3 %collective-permute-done.8 = f32[1024]{0:T(1024)S(1)} collective-permute-done((f32[1024]{0:T(1024)S(1)}, f32[1024]{0:T(1024)S(1)}, u32[]{:S(2)}, u32[]{:S(2)}) %collective-permute-start.8) | collective-permute-done | bytes 4128 | tf_op jit(solution)/shard_map/ppermute | solution.py:19
  83.4 5.6 %add_reduce_fusion.1 = f32[1024]{0:T(1024)S(1)} fusion(f32[3072]{0:T(1024)S(1)} %pad_maximum_fusion.5, f32[1024,1024]{1,0:T(8,128)} %multiply_bitcast_fusion, f32[1024,2048]{1,0:T(8,128)} %convolution_multiply_fusion), kind=kLoop, calls=%fused_computation.12 | loop fusion | flops 9436160 | bytes 12599296 | tf_op jit(solution)/shard_map/reduce_max | solution.py:23
  88.9 6.3 %exponential_reduce_fusion.2 = f32[1024]{0:T(1024)S(1)} fusion(f32[1024]{0:T(1024)S(1)} %add_reduce_fusion.1, f32[3072]{0:T(1024)S(1)} %pad_maximum_fusion.5, f32[1024,1024]{1,0:T(8,128)} %multiply_bitcast_fusion, f32[1024,2048]{1,0:T(8,128)} %convolution_multiply_fusion), kind=kLoop, calls=%fused_computation.8 | loop fusion | flops 12581888 | bytes 12603392 | tf_op jit(solution)/shard_map/reduce_sum | solution.py:24
  101.7 5.9 %add_reduce_fusion = f32[3072]{0:T(1024)S(1)} fusion(f32[1024]{0:T(1024)S(1)} %add_subtract_fusion.1, f32[1024,1024]{1,0:T(8,128)} %multiply_bitcast_fusion, f32[1024,2048]{1,0:T(8,128)} %convolution_multiply_fusion), kind=kLoop, calls=%fused_computation.11 | loop fusion | flops 9434112 | bytes 12599296 | tf_op jit(solution)/shard_map/reduce_max | solution.py:28
  107.6 5.3 %exponential_reduce_fusion.1 = f32[3072]{0:T(1024)S(1)} fusion(f32[3072]{0:T(1024)S(1)} %add_reduce_fusion, f32[1024]{0:T(1024)S(1)} %add_subtract_fusion.1, f32[1024,1024]{1,0:T(8,128)S(1)} %copy-done.2, f32[1024,2048]{1,0:T(8,128)} %convolution_multiply_fusion), kind=kLoop, calls=%fused_computation.7 | loop fusion | flops 12579840 | bytes 12611584 | tf_op jit(solution)/shard_map/reduce_sum | solution.py:29
  115.5 5.6 %collective-permute-done.12 = f32[1024]{0:T(1024)S(1)} collective-permute-done((f32[1024]{0:T(1024)S(1)}, f32[1024]{0:T(1024)S(1)}, u32[]{:S(2)}, u32[]{:S(2)}) %collective-permute-start.12) | collective-permute-done | bytes 4128 | tf_op jit(solution)/shard_map/ppermute | solution.py:19
  122.5 5.2 %collective-permute-done.15 = f32[1024]{0:T(1024)S(1)} collective-permute-done((f32[1024]{0:T(1024)S(1)}, f32[1024]{0:T(1024)S(1)}, u32[]{:S(2)}, u32[]{:S(2)}) %collective-permute-start.15) | collective-permute-done | bytes 4128 | tf_op jit(solution)/shard_map/ppermute | solution.py:19
  127.7 5.6 %add_reduce_fusion.4 = f32[1024]{0:T(1024)S(1)} fusion(f32[3072]{0:T(1024)S(1)} %pad_maximum_fusion.6, f32[1024,1024]{1,0:T(8,128)} %multiply_bitcast_fusion, f32[1024,2048]{1,0:T(8,128)} %convolution_multiply_fusion), kind=kLoop, calls=%fused_computation.15 | loop fusion | flops 9436160 | bytes 12599296 | tf_op jit(solution)/shard_map/reduce_max | solution.py:23
  133.3 6.3 %exponential_reduce_fusion = f32[1024]{0:T(1024)S(1)} fusion(f32[1024]{0:T(1024)S(1)} %add_reduce_fusion.4, f32[3072]{0:T(1024)S(1)} %pad_maximum_fusion.6, f32[1024,1024]{1,0:T(8,128)} %multiply_bitcast_fusion, f32[1024,2048]{1,0:T(8,128)} %convolution_multiply_fusion), kind=kLoop, calls=%fused_computation.6 | loop fusion | flops 12581888 | bytes 12603392 | tf_op jit(solution)/shard_map/reduce_sum | solution.py:24
  145.9 6.4 %exponential_convert_fusion = bf16[1024,3072]{1,0:T(8,128)(2,1)S(1)} fusion(f32[1024]{0:T(1024)S(1)} %get-tuple-element.4, f32[3072]{0:T(1024)S(1)} %pad_maximum_fusion.6, f32[1024,1024]{1,0:T(8,128)} %multiply_bitcast_fusion, f32[1024,2048]{1,0:T(8,128)} %convolution_multiply_fusion), kind=kLoop, calls=%fused_computation.5 | loop fusion | flops 12582912 | bytes 18890752 | tf_op jit(solution)/shard_map/convert_element_type | solution.py:113
  152.3 3.4 %fusion = f32[1024,768]{1,0:T(8,128)S(1)} fusion(bf16[2048,768]{1,0:T(8,128)(2,1)S(1)} %copy-done.3, bf16[1024,3072]{1,0:T(8,128)(2,1)S(1)} %exponential_convert_fusion), kind=kOutput, calls=%fused_computation.17 | convolution fusion | flops 3221225472 | bytes 10485760 | tf_op jit(solution)/shard_map/dot_general | solution.py:114
  164.2 17.6 %collective-permute-done.21 = f32[256,768]{1,0:T(8,128)S(1)} collective-permute-done((f32[256,768]{1,0:T(8,128)}, f32[256,768]{1,0:T(8,128)S(1)}, u32[]{:S(2)}, u32[]{:S(2)}) %collective-permute-start.21) | collective-permute-done | bytes 786464 | tf_op jit(solution)/shard_map/ppermute | solution.py:19
  184.4 14.9 %collective-permute-done.19 = f32[256,768]{1,0:T(8,128)} collective-permute-done((f32[256,768]{1,0:T(8,128)S(1)}, f32[256,768]{1,0:T(8,128)}, u32[]{:S(2)}, u32[]{:S(2)}) %collective-permute-start.19) | collective-permute-done | bytes 786464 | tf_op jit(solution)/shard_map/ppermute | solution.py:19
  202.6 8.8 %collective-permute-done.24 = bf16[256,768]{1,0:T(8,128)(2,1)S(1)} collective-permute-done((bf16[256,768]{1,0:T(8,128)(2,1)S(1)}, bf16[256,768]{1,0:T(8,128)(2,1)S(1)}, u32[]{:S(2)}, u32[]{:S(2)}) %collective-permute-start.24) | collective-permute-done | bytes 393248 | tf_op jit(solution)/shard_map/ppermute | solution.py:19
  213.1 9.1 %collective-permute-done.22 = bf16[256,768]{1,0:T(8,128)(2,1)S(1)} collective-permute-done((bf16[256,768]{1,0:T(8,128)(2,1)S(1)}, bf16[256,768]{1,0:T(8,128)(2,1)S(1)}, u32[]{:S(2)}, u32[]{:S(2)}) %collective-permute-start.22) | collective-permute-done | bytes 393248 | tf_op jit(solution)/shard_map/ppermute | solution.py:19
  (100 shorter events, 50.6 us)
Async XLA Ops:
  9.3 17.7 %collective-permute-start = (bf16[1024,768]{1,0:T(8,128)(2,1)}, bf16[1024,768]{1,0:T(8,128)(2,1)}, u32[]{:S(2)}, u32[]{:S(2)}) collective-permute-start(bf16[1024,768]{1,0:T(8,128)(2,1)} %get-tuple-element.13), channel_id=1, source_target_pairs={{0,4},{4,8},{8,12},{12,16},{16,20},{20,24},{24,28},{28,32},{32,36}... | collective-permute-start | bytes 4718600 | tf_op jit(solution)/shard_map/ppermute | solution.py:19
  9.3 23.3 %collective-permute-start.1 = (bf16[1024,768]{1,0:T(8,128)(2,1)S(1)}, bf16[1024,768]{1,0:T(8,128)(2,1)}, u32[]{:S(2)}, u32[]{:S(2)}) collective-permute-start(bf16[1024,768]{1,0:T(8,128)(2,1)S(1)} %get-tuple-element.12), channel_id=1, source_target_pairs={{0,124},{4,0},{8,4},{12,8},{16,12},{20,16},{24,20},{28,24},{32,28}... | collective-permute-start | bytes 4718600 | tf_op jit(solution)/shard_map/ppermute | solution.py:19
  49.7 6.2 %collective-permute-start.4 = (f32[1024]{0:T(1024)S(1)}, f32[1024]{0:T(1024)S(1)}, u32[]{:S(2)}, u32[]{:S(2)}) collective-permute-start(f32[1024]{0:T(1024)S(1)} %log_add_fusion.5), channel_id=1, source_target_pairs={{0,3},{1,0},{2,1},{3,2},{4,7},{5,4},{6,5},{7,6},{8,11},{9,8},{10,9... | collective-permute-start | bytes 12296 | tf_op jit(solution)/shard_map/ppermute | solution.py:19
  52.3 4.0 %collective-permute-start.3 = (f32[1024]{0:T(1024)S(1)}, f32[1024]{0:T(1024)S(1)}, u32[]{:S(2)}, u32[]{:S(2)}) collective-permute-start(f32[1024]{0:T(1024)S(1)} %log_add_fusion.5), channel_id=1, source_target_pairs={{0,2},{1,3},{2,0},{3,1},{4,6},{5,7},{6,4},{7,5},{8,10},{9,11},{10,... | collective-permute-start | bytes 12296 | tf_op jit(solution)/shard_map/ppermute | solution.py:19
  52.8 3.7 %collective-permute-start.2 = (f32[1024]{0:T(1024)S(1)}, f32[1024]{0:T(1024)S(1)}, u32[]{:S(2)}, u32[]{:S(2)}) collective-permute-start(f32[1024]{0:T(1024)S(1)} %log_add_fusion.5), channel_id=1, source_target_pairs={{0,1},{1,2},{2,3},{3,0},{4,5},{5,6},{6,7},{7,4},{8,9},{9,10},{10,1... | collective-permute-start | bytes 12296 | tf_op jit(solution)/shard_map/ppermute | solution.py:19
  68.4 2.7 %collective-permute-start.6 = (f32[1024]{0:T(1024)S(1)}, f32[1024]{0:T(1024)S(1)}, u32[]{:S(2)}, u32[]{:S(2)}) collective-permute-start(f32[1024]{0:T(1024)S(1)} %slice_select_fusion.1), channel_id=1, source_target_pairs={{0,4},{4,8},{8,12},{12,16},{16,20},{20,24},{24,28},{28,32},{32,36}... | collective-permute-start | bytes 12296 | tf_op jit(solution)/shard_map/ppermute | solution.py:19
  70.4 6.4 %collective-permute-start.5 = (f32[1024]{0:T(1024)S(1)}, f32[1024]{0:T(1024)S(1)}, u32[]{:S(2)}, u32[]{:S(2)}) collective-permute-start(f32[1024]{0:T(1024)S(1)} %slice_select_fusion.1), channel_id=1, source_target_pairs={{0,124},{4,0},{8,4},{12,8},{16,12},{20,16},{24,20},{28,24},{32,28}... | collective-permute-start | bytes 12296 | tf_op jit(solution)/shard_map/ppermute | solution.py:19
  77.0 6.4 %collective-permute-start.8 = (f32[1024]{0:T(1024)S(1)}, f32[1024]{0:T(1024)S(1)}, u32[]{:S(2)}, u32[]{:S(2)}) collective-permute-start(f32[1024]{0:T(1024)S(1)} %bitcast.62), channel_id=1, source_target_pairs={{0,124},{4,0},{8,4},{12,8},{16,12},{20,16},{24,20},{28,24},{32,28}... | collective-permute-start | bytes 12296 | tf_op jit(solution)/shard_map/ppermute | solution.py:19
  95.3 2.5 %collective-permute-start.11 = (f32[1024]{0:T(1024)S(1)}, f32[1024]{0:T(1024)S(1)}, u32[]{:S(2)}, u32[]{:S(2)}) collective-permute-start(f32[1024]{0:T(1024)S(1)} %log_add_fusion.4), channel_id=1, source_target_pairs={{0,3},{1,0},{2,1},{3,2},{4,7},{5,4},{6,5},{7,6},{8,11},{9,8},{10,9... | collective-permute-start | bytes 12296 | tf_op jit(solution)/shard_map/ppermute | solution.py:19
  96.1 4.0 %collective-permute-start.10 = (f32[1024]{0:T(1024)S(1)}, f32[1024]{0:T(1024)S(1)}, u32[]{:S(2)}, u32[]{:S(2)}) collective-permute-start(f32[1024]{0:T(1024)S(1)} %log_add_fusion.4), channel_id=1, source_target_pairs={{0,2},{1,3},{2,0},{3,1},{4,6},{5,7},{6,4},{7,5},{8,10},{9,11},{10,... | collective-permute-start | bytes 12296 | tf_op jit(solution)/shard_map/ppermute | solution.py:19
  97.3 3.7 %collective-permute-start.9 = (f32[1024]{0:T(1024)S(1)}, f32[1024]{0:T(1024)S(1)}, u32[]{:S(2)}, u32[]{:S(2)}) collective-permute-start(f32[1024]{0:T(1024)S(1)} %log_add_fusion.4), channel_id=1, source_target_pairs={{0,1},{1,2},{2,3},{3,0},{4,5},{5,6},{6,7},{7,4},{8,9},{9,10},{10,1... | collective-permute-start | bytes 12296 | tf_op jit(solution)/shard_map/ppermute | solution.py:19
  112.9 2.6 %collective-permute-start.13 = (f32[1024]{0:T(1024)S(1)}, f32[1024]{0:T(1024)S(1)}, u32[]{:S(2)}, u32[]{:S(2)}) collective-permute-start(f32[1024]{0:T(1024)S(1)} %slice_select_fusion), channel_id=1, source_target_pairs={{0,4},{4,8},{8,12},{12,16},{16,20},{20,24},{24,28},{28,32},{32,36}... | collective-permute-start | bytes 12296 | tf_op jit(solution)/shard_map/ppermute | solution.py:19
  114.7 6.4 %collective-permute-start.12 = (f32[1024]{0:T(1024)S(1)}, f32[1024]{0:T(1024)S(1)}, u32[]{:S(2)}, u32[]{:S(2)}) collective-permute-start(f32[1024]{0:T(1024)S(1)} %slice_select_fusion), channel_id=1, source_target_pairs={{0,124},{4,0},{8,4},{12,8},{16,12},{20,16},{24,20},{28,24},{32,28}... | collective-permute-start | bytes 12296 | tf_op jit(solution)/shard_map/ppermute | solution.py:19
  121.2 1.3 collective-permute-start.14
  121.3 6.4 %collective-permute-start.15 = (f32[1024]{0:T(1024)S(1)}, f32[1024]{0:T(1024)S(1)}, u32[]{:S(2)}, u32[]{:S(2)}) collective-permute-start(f32[1024]{0:T(1024)S(1)} %bitcast.60), channel_id=1, source_target_pairs={{0,124},{4,0},{8,4},{12,8},{16,12},{20,16},{24,20},{28,24},{32,28}... | collective-permute-start | bytes 12296 | tf_op jit(solution)/shard_map/ppermute | solution.py:19
  139.6 2.5 %collective-permute-start.18 = (f32[1024]{0:T(1024)S(1)}, f32[1024]{0:T(1024)S(1)}, u32[]{:S(2)}, u32[]{:S(2)}) collective-permute-start(f32[1024]{0:T(1024)S(1)} %log_add_fusion.3), channel_id=1, source_target_pairs={{0,3},{1,0},{2,1},{3,2},{4,7},{5,4},{6,5},{7,6},{8,11},{9,8},{10,9... | collective-permute-start | bytes 12296 | tf_op jit(solution)/shard_map/ppermute | solution.py:19
  140.4 4.0 %collective-permute-start.17 = (f32[1024]{0:T(1024)S(1)}, f32[1024]{0:T(1024)S(1)}, u32[]{:S(2)}, u32[]{:S(2)}) collective-permute-start(f32[1024]{0:T(1024)S(1)} %log_add_fusion.3), channel_id=1, source_target_pairs={{0,2},{1,3},{2,0},{3,1},{4,6},{5,7},{6,4},{7,5},{8,10},{9,11},{10,... | collective-permute-start | bytes 12296 | tf_op jit(solution)/shard_map/ppermute | solution.py:19
  141.0 3.7 %collective-permute-start.16 = (f32[1024]{0:T(1024)S(1)}, f32[1024]{0:T(1024)S(1)}, u32[]{:S(2)}, u32[]{:S(2)}) collective-permute-start(f32[1024]{0:T(1024)S(1)} %log_add_fusion.3), channel_id=1, source_target_pairs={{0,1},{1,2},{2,3},{3,0},{4,5},{5,6},{6,7},{7,4},{8,9},{9,10},{10,1... | collective-permute-start | bytes 12296 | tf_op jit(solution)/shard_map/ppermute | solution.py:19
  161.9 19.9 %collective-permute-start.21 = (f32[256,768]{1,0:T(8,128)}, f32[256,768]{1,0:T(8,128)S(1)}, u32[]{:S(2)}, u32[]{:S(2)}) collective-permute-start(f32[256,768]{1,0:T(8,128)} %get-tuple-element.10), channel_id=1, source_target_pairs={{0,3},{1,0},{2,1},{3,2},{4,7},{5,4},{6,5},{7,6},{8,11},{9,8},{10,9... | collective-permute-start | bytes 2359304 | tf_op jit(solution)/shard_map/ppermute | solution.py:19
  163.3 21.1 %collective-permute-start.20 = (f32[256,768]{1,0:T(8,128)}, f32[256,768]{1,0:T(8,128)}, u32[]{:S(2)}, u32[]{:S(2)}) collective-permute-start(f32[256,768]{1,0:T(8,128)} %get-tuple-element.11), channel_id=1, source_target_pairs={{0,2},{1,3},{2,0},{3,1},{4,6},{5,7},{6,4},{7,5},{8,10},{9,11},{10,... | collective-permute-start | bytes 2359304 | tf_op jit(solution)/shard_map/ppermute | solution.py:19
  164.2 35.1 %collective-permute-start.19 = (f32[256,768]{1,0:T(8,128)S(1)}, f32[256,768]{1,0:T(8,128)}, u32[]{:S(2)}, u32[]{:S(2)}) collective-permute-start(f32[256,768]{1,0:T(8,128)S(1)} %get-tuple-element.9), channel_id=1, source_target_pairs={{0,1},{1,2},{2,3},{3,0},{4,5},{5,6},{6,7},{7,4},{8,9},{9,10},{10,1... | collective-permute-start | bytes 2359304 | tf_op jit(solution)/shard_map/ppermute | solution.py:19
  201.1 10.3 %collective-permute-start.24 = (bf16[256,768]{1,0:T(8,128)(2,1)S(1)}, bf16[256,768]{1,0:T(8,128)(2,1)S(1)}, u32[]{:S(2)}, u32[]{:S(2)}) collective-permute-start(bf16[256,768]{1,0:T(8,128)(2,1)S(1)} %add_convert_fusion), channel_id=1, source_target_pairs={{0,3},{1,0},{2,1},{3,2},{4,7},{5,4},{6,5},{7,6},{8,11},{9,8},{10,9... | collective-permute-start | bytes 1179656 | tf_op jit(solution)/shard_map/ppermute | solution.py:19
  201.3 11.9 %collective-permute-start.23 = (bf16[256,768]{1,0:T(8,128)(2,1)S(1)}, bf16[256,768]{1,0:T(8,128)(2,1)S(1)}, u32[]{:S(2)}, u32[]{:S(2)}) collective-permute-start(bf16[256,768]{1,0:T(8,128)(2,1)S(1)} %add_convert_fusion), channel_id=1, source_target_pairs={{0,2},{1,3},{2,0},{3,1},{4,6},{5,7},{6,4},{7,5},{8,10},{9,11},{10,... | collective-permute-start | bytes 1179656 | tf_op jit(solution)/shard_map/ppermute | solution.py:19
  201.9 20.3 %collective-permute-start.22 = (bf16[256,768]{1,0:T(8,128)(2,1)S(1)}, bf16[256,768]{1,0:T(8,128)(2,1)S(1)}, u32[]{:S(2)}, u32[]{:S(2)}) collective-permute-start(bf16[256,768]{1,0:T(8,128)(2,1)S(1)} %add_convert_fusion), channel_id=1, source_target_pairs={{0,1},{1,2},{2,3},{3,0},{4,5},{5,6},{6,7},{7,4},{8,9},{9,10},{10,1... | collective-permute-start | bytes 1179656 | tf_op jit(solution)/shard_map/ppermute | solution.py:19
  (6 other events, 35.4 us)

commit v2 on v1

--- a/solution.py
+++ b/solution.py
@@ -4,6 +4,7 @@
 import jax.numpy as jnp
 from jax import lax
 from jax.sharding import PartitionSpec as P
+from jax.experimental import pallas as pl
 
 BLK = 1024
 ITERS = 2
@@ -19,14 +20,89 @@
     return lax.ppermute(x, axis, route)
 
 
-def lse_rows(scores):
-    top = jnp.max(scores, axis=1)
-    return top + jnp.log(jnp.sum(jnp.exp(scores - top[:, None]), axis=1))
-
-
-def lse_cols(scores):
-    top = jnp.max(scores, axis=0)
-    return top + jnp.log(jnp.sum(jnp.exp(scores - top[None, :]), axis=0))
+def _row_kernel(*refs):
+    n = (len(refs) - 1) // 2
+    out_ref = refs[-1]
+    scores = [refs[k][...] + refs[n + k][...] for k in range(n)]
+    top = scores[0].max(axis=1, keepdims=True)
+    for s in scores[1:]:
+        top = jnp.maximum(top, s.max(axis=1, keepdims=True))
+    total = jnp.sum(jnp.exp(scores[0] - top), axis=1, keepdims=True)
+    for s in scores[1:]:
+        total = total + jnp.sum(jnp.exp(s - top), axis=1, keepdims=True)
+    out_ref[...] = top + jnp.log(total)
+
+
+def row_lse_call(zs, gs, tm=256):
+    rows = zs[0].shape[0]
+    in_specs = [pl.BlockSpec((tm, z.shape[1]), lambda i: (i, 0)) for z in zs]
+    in_specs += [pl.BlockSpec((1, g.shape[1]), lambda i: (0, 0)) for g in gs]
+    return pl.pallas_call(
+        _row_kernel,
+        grid=(rows // tm,),
+        in_specs=in_specs,
+        out_specs=pl.BlockSpec((tm, 1), lambda i: (i, 0)),
+        out_shape=jax.ShapeDtypeStruct((rows, 1), jnp.float32),
+    )(*zs, *gs)
+
+
+def _col_kernel(zo_ref, ze_ref, f_ref, oo_ref, oe_ref):
+    f = f_ref[...]
+    for z_ref, o_ref in ((zo_ref, oo_ref), (ze_ref, oe_ref)):
+        s = z_ref[...] + f
+        top = s.max(axis=0, keepdims=True)
+        o_ref[...] = top + jnp.log(jnp.sum(jnp.exp(s - top), axis=0, keepdims=True))
+
+
+def col_lse_call(zo, ze, f, steps=4):
+    rows = zo.shape[0]
+    wo = zo.shape[1] // steps
+    we = ze.shape[1] // steps
+    return pl.pallas_call(
+        _col_kernel,
+        grid=(steps,),
+        in_specs=[
+            pl.BlockSpec((rows, wo), lambda j: (0, j)),
+            pl.BlockSpec((rows, we), lambda j: (0, j)),
+            pl.BlockSpec((rows, 1), lambda j: (0, 0)),
+        ],
+        out_specs=[
+            pl.BlockSpec((1, wo), lambda j: (0, j)),
+            pl.BlockSpec((1, we), lambda j: (0, j)),
+        ],
+        out_shape=[
+            jax.ShapeDtypeStruct((1, zo.shape[1]), jnp.float32),
+            jax.ShapeDtypeStruct((1, ze.shape[1]), jnp.float32),
+        ],
+    )(zo, ze, f)
+
+
+def _map_kernel(zo_ref, ze_ref, go_ref, ge_ref, l_ref, to_ref, te_ref, out_ref):
+    lse = l_ref[...]
+    wo = jnp.exp(zo_ref[...] + go_ref[...] - lse).astype(jnp.bfloat16)
+    we = jnp.exp(ze_ref[...] + ge_ref[...] - lse).astype(jnp.bfloat16)
+    acc = jnp.dot(wo, to_ref[...], preferred_element_type=jnp.float32)
+    out_ref[...] = acc + jnp.dot(we, te_ref[...], preferred_element_type=jnp.float32)
+
+
+def map_call(zo, ze, go, ge, lse, to, te, tm=256):
+    rows = zo.shape[0]
+    feats = to.shape[1]
+    return pl.pallas_call(
+        _map_kernel,
+        grid=(rows // tm,),
+        in_specs=[
+            pl.BlockSpec((tm, zo.shape[1]), lambda i: (i, 0)),
+            pl.BlockSpec((tm, ze.shape[1]), lambda i: (i, 0)),
+            pl.BlockSpec((1, go.shape[1]), lambda i: (0, 0)),
+            pl.BlockSpec((1, ge.shape[1]), lambda i: (0, 0)),
+            pl.BlockSpec((tm, 1), lambda i: (i, 0)),
+            pl.BlockSpec(to.shape, lambda i: (0, 0)),
+            pl.BlockSpec(te.shape, lambda i: (0, 0)),
+        ],
+        out_specs=pl.BlockSpec((tm, feats), lambda i: (i, 0)),
+        out_shape=jax.ShapeDtypeStruct((rows, feats), jnp.float32),
+    )(zo, ze, go, ge, lse, to, te)
 
 
 def narrow_lse(partial_value, column, narrow_count):
@@ -70,29 +146,35 @@
     from_left = shifted(to_right, "wide", 1)
     from_right = shifted(to_left, "wide", -1)
 
-    own = lax.dot_general(
+    zo = lax.dot_general(
         sources, targets, (((1,), (1,)), ((), ())), preferred_element_type=jnp.float32
     ) * scale
     extra = jnp.where(mine_from_left, from_left, from_right)
-    extra_dots = lax.dot_general(
+    ze = lax.dot_general(
         sources, extra, (((1,), (1,)), ((), ())), preferred_element_type=jnp.float32
     ) * scale
-    z = jnp.concatenate([own, extra_dots], axis=1)
 
     extra_mask = jnp.where(mine_live, 0.0, sentinel).astype(jnp.float32)
-
-    def row_lse(g_own, g_extra):
-        gs = jnp.concatenate([g_own * inv_eps, g_extra * inv_eps + extra_mask])
-        return narrow_lse(lse_rows(z + gs[None, :]), c, narrow_count)
-
-    g_own = jnp.zeros((tgt_blocks * BLK,), jnp.float32)
+    own_width = tgt_blocks * BLK
+
+    def scaled(g_own, g_extra):
+        return ((g_own * inv_eps).reshape(1, own_width), (g_extra * inv_eps + extra_mask).reshape(1, BLK))
+
+    g_own = jnp.zeros((own_width,), jnp.float32)
     g_extra = jnp.zeros((BLK,), jnp.float32)
     for iteration in range(ITERS):
-        row = row_lse(g_own, g_extra)
+        go, ge = scaled(g_own, g_extra)
+        if iteration == 0:
+            part_own = row_lse_call([zo], [go])
+            part_ext = row_lse_call([ze], [ge])
+            part = jnp.logaddexp(part_own, part_ext)
+        else:
+            part = row_lse_call([zo, ze], [go, ge])
+        row = narrow_lse(part.reshape(-1), c, narrow_count)
         f = epsilon * (log_src - row)
-        cols = lse_cols(z + (f * inv_eps)[:, None])
-        own_cols = cols[: tgt_blocks * BLK].reshape(tgt_blocks, BLK)
-        extra_cols = jnp.where(mine_live, cols[tgt_blocks * BLK:], sentinel)
+        own_cols, extra_cols = col_lse_call(zo, ze, (f * inv_eps).reshape(-1, 1))
+        own_cols = own_cols.reshape(tgt_blocks, BLK)
+        extra_cols = jnp.where(mine_live, extra_cols.reshape(-1), sentinel)
         back_from_right = shifted(extra_cols, "wide", -1)
         back_from_left = shifted(extra_cols, "wide", 1)
         ids = jnp.arange(tgt_blocks, dtype=jnp.int32)[:, None]
@@ -107,12 +189,10 @@
         send_left = g_blocks[want_left % tgt_blocks]
         g_extra = jnp.where(mine_from_left, shifted(send_right, "wide", 1), shifted(send_left, "wide", -1))
 
-    row = row_lse(g_own, g_extra)
+    go, ge = scaled(g_own, g_extra)
+    row = narrow_lse(row_lse_call([zo, ze], [go, ge]).reshape(-1), c, narrow_count)
     source_pot = epsilon * (log_src - row)
-    gs = jnp.concatenate([g_own * inv_eps, g_extra * inv_eps + extra_mask])
-    weights = jnp.exp(z + gs[None, :] - row[:, None]).astype(jnp.bfloat16)
-    numer = jnp.dot(weights[:, : tgt_blocks * BLK], targets, preferred_element_type=jnp.float32)
-    numer = numer + jnp.dot(weights[:, tgt_blocks * BLK:], extra, preferred_element_type=jnp.float32)
+    numer = map_call(zo, ze, go, ge, row.reshape(-1, 1), targets, extra)
 
     rows = sources.shape[0]
     part = rows // narrow_count

time: 225 us -> 212 us (0.942)
  other arithmetic: 68.2 us -> 14.6 us
  Pallas kernels: 0 us -> 50.6 us
  matrix products: 19.4 us -> 11.3 us
  waiting for transfers between devices: 96.3 us -> 90.6 us
  local copies, waits for them, and re-layouts: 12.7 us -> 17.4 us
    pallas_call x0 -> x7, Pallas kernels: none -> 50.6 us  [the longest x4 24.5 us: row_lse_call(): pl.pallas_call(_row_kernel, grid=(rows // tm,), in_specs=in_specs, out_sp...]
    reduce_sum x5 -> x0, other arithmetic: 29.6 us -> none  [the longest x3 19 us: lse_rows(): return top + jnp.log(jnp.sum(jnp.exp(scores - top[:, None]), axis=1))]
    reduce_max x5 -> x0, other arithmetic: 28.4 us -> none  [the longest x3 16.7 us: lse_rows(): top = jnp.max(scores, axis=1)]
    dot_general x2 -> x0, matrix products: 6.67 us -> none  [the longest x1 3.42 us: shards(): jnp.dot(weights[:, :tgt_blocks * BLK], targets, preferred_element_type=jn...]
    pallas_call x0 -> x4, other arithmetic: none -> 6.45 us  [the longest x2 3.96 us: col_lse_call(): pl.pallas_call(_col_kernel, grid=(steps,), in_specs=[pl.BlockSpec((rows,...]
    convert_element_type x1 -> x0, other arithmetic: 6.35 us -> none  [shards(): weights = jnp.exp(z + gs[None, :] - row[:, None]).astype(jnp.bfloat16)]
    ppermute x25, waiting for transfers between devices: 96.3 us -> 90.6 us  [shifted(): return lax.ppermute(x, axis, route)]
    select_n x2 -> x4, other arithmetic: 0.01 us -> 3.01 us  [the longest x1 1.46 us: shards(): part = jnp.logaddexp(part_own, part_ext)]
  transfers between devices with their start and end apart: 25 -> 25, of which waited for: 23 -> 22; matrix products, arithmetic and copies ran while one was open for 4% -> 5% of each run, Pallas kernels for 0% -> 3%
where the time goes in v2:
time: 212 us; the launch traced here: 211 us
  waiting for transfers between devices  90.6 us (43%)
  Pallas kernels  50.6 us (24%)
  local copies, waits for them, and re-layouts  17.4 us (8%)
  starting transfers between devices  16.2 us (8%)
  other arithmetic  14.6 us (7%)
  matrix products  11.3 us (5%)
  between operations  10.5 us (5%)
    ppermute x25, waiting for transfers between devices, shifted(): return lax.ppermute(x, axis, route)  90.6 us
    pallas_call x4, Pallas kernels, row_lse_call(): pl.pallas_call(_row_kernel, grid=(rows // tm,), in_specs=in_specs, out_sp...  24.5 us
    ppermute x25, starting transfers between devices, shifted(): return lax.ppermute(x, axis, route)  16.2 us
    pallas_call x2, Pallas kernels, col_lse_call(): pl.pallas_call(_col_kernel, grid=(steps,), in_specs=[pl.BlockSpec((rows,...  14.8 us
    pallas_call x1, Pallas kernels, map_call(): pl.pallas_call(_map_kernel, grid=(rows // tm,), in_specs=[pl.BlockSpec((t...  11.3 us
    dot_general x1, matrix products, shards(): lax.dot_general(sources, targets, (((1,), (1,)), ((), ())), preferred_ele...  7.54 us
  transfers between devices with their start and end apart: 25, of which 22 were waited for; matrix products, arithmetic and copies ran while one was open for 5% of the time, Pallas kernels for 3%

profile of v2, /device:TPU:121, one launch (start us, length us, event | category | flops | bytes accessed | tf_op | source)
XLA Modules:
  0.0 211.2 jit_solution(1764434028801664873)
XLA Ops:
  6.0 3.8 %dynamic-slice_bitcast_fusion = (bf16[1024,768]{1,0:T(8,128)(2,1)}, bf16[1024,768]{1,0:T(8,128)(2,1)}) fusion(bf16[2,1024,768]{2,1,0:T(8,128)(2,1)} %bitcast.110, s32[]{:T(128)S(6)} %select_n.259, s32[]{:T(128)S(6)} %select_n.256), kind=kLoop, calls=%fused_computation.7 | loop fusion | bytes 6291464 | tf_op jit(solution)/shard_map/squeeze | solution.py:145
  14.4 7.5 %convolution_multiply_fusion.refs_0_.zo_ref = f32[1024,2048]{1,0:T(8,128)} fusion(bf16[1024,768]{1,0:T(8,128)(2,1)S(1)} %copy-done, bf16[2048,768]{1,0:T(8,128)(2,1)} %to_ref.1), kind=kOutput, calls=%fused_computation.4 | convolution fusion | flops 3223322624 | bytes 13107200 | tf_op jit(solution)/shard_map/dot_general | solution.py:149
  22.6 5.8 %shard_map.67 = f32[1024,1]{1,0:T(8,128)} custom-call(f32[1024,2048]{1,0:T(8,128)} %convolution_multiply_fusion.refs_0_.zo_ref, f32[1,2048]{1,0:T(1,128)} %reshape.305.refs_1_), custom_call_target="tpu_custom_call" | custom-call | tf_op jit(solution)/shard_map/pallas_call | solution.py:40
  28.4 4.9 %collective-permute-done.1 = bf16[1024,768]{1,0:T(8,128)(2,1)} collective-permute-done((bf16[1024,768]{1,0:T(8,128)(2,1)}, bf16[1024,768]{1,0:T(8,128)(2,1)}, u32[]{:S(2)}, u32[]{:S(2)}) %collective-permute-start.1) | collective-permute-done | bytes 1572896 | tf_op jit(solution)/shard_map/ppermute | solution.py:20
  33.5 3.8 %multiply_bitcast_fusion.refs_0_.ze_ref.refs_1_ = f32[1024,1024]{1,0:T(8,128)} fusion(bf16[1024,768]{1,0:T(8,128)(2,1)S(1)} %broadcast_select_fusion.te_ref, bf16[1024,768]{1,0:T(8,128)(2,1)S(1)} %copy-done), kind=kOutput, calls=%fused_computation.5 | convolution fusion | flops 1611661312 | bytes 7340032 | tf_op jit(solution)/shard_map/dot_general | solution.py:153
  37.9 4.5 %shard_map.68 = f32[1024,1]{1,0:T(8,128)} custom-call(f32[1024,1024]{1,0:T(8,128)} %multiply_bitcast_fusion.refs_0_.ze_ref.refs_1_, f32[1,1024]{1,0:T(1,128)} %reshape.306.refs_1_), custom_call_target="tpu_custom_call" | custom-call | tf_op jit(solution)/shard_map/pallas_call | solution.py:40
  43.8 3.9 %collective-permute-start.4 = (f32[1024]{0:T(1024)S(1)}, f32[1024]{0:T(1024)S(1)}, u32[]{:S(2)}, u32[]{:S(2)}) collective-permute-start(f32[1024]{0:T(1024)S(1)} %select_reduce_fusion), channel_id=1, source_target_pairs={{0,3},{1,0},{2,1},{3,2},{4,7},{5,4},{6,5},{7,6},{8,11},{9,8},{10,9... | collective-permute-start | bytes 12296 | tf_op jit(solution)/shard_map/ppermute | solution.py:20
  53.4 7.4 %shard_map.69 = (f32[1,2048]{1,0:T(1,128)}, f32[1,1024]{1,0:T(1,128)}) custom-call(f32[1024,2048]{1,0:T(8,128)} %convolution_multiply_fusion.refs_0_.zo_ref, f32[1024,1024]{1,0:T(8,128)} %multiply_bitcast_fusion.refs_0_.ze_ref.refs_1_, f32[1024,1]{1,0:T(8,128)} %copy.13.f_ref), custom_call_target="tpu_custom_call" | custom-call | tf_op jit(solution)/shard_map/pallas_call | solution.py:61
  63.7 5.5 %collective-permute-done.5 = f32[1024]{0:T(1024)S(1)} collective-permute-done((f32[1024]{0:T(1024)S(1)}, f32[1024]{0:T(1024)S(1)}, u32[]{:S(2)}, u32[]{:S(2)}) %collective-permute-start.5) | collective-permute-done | bytes 4128 | tf_op jit(solution)/shard_map/ppermute | solution.py:20
  69.8 2.0 fusion.24
  73.2 5.3 %collective-permute-done.8 = f32[1024]{0:T(1024)S(1)} collective-permute-done((f32[1024]{0:T(1024)S(1)}, f32[1024]{0:T(1024)S(1)}, u32[]{:S(2)}, u32[]{:S(2)}) %collective-permute-start.8) | collective-permute-done | bytes 4128 | tf_op jit(solution)/shard_map/ppermute | solution.py:20
  79.1 7.1 %shard_map.70 = f32[1024,1]{1,0:T(8,128)} custom-call(f32[1024,2048]{1,0:T(8,128)} %convolution_multiply_fusion.refs_0_.zo_ref, f32[1024,1024]{1,0:T(8,128)} %multiply_bitcast_fusion.refs_0_.ze_ref.refs_1_, f32[1,2048]{1,0:T(1,128)} %get-tuple-element.25.refs_2_, f32[1,1024]{1,0:T(1,128)} %bitcast.125), custom_call_target="tpu_custom_call" | custom-call | tf_op jit(solution)/shard_map/pallas_call | solution.py:40
  90.0 2.2 %collective-permute-done.10 = f32[1024]{0:T(1024)S(1)} collective-permute-done((f32[1024]{0:T(1024)S(1)}, f32[1024]{0:T(1024)S(1)}, u32[]{:S(2)}, u32[]{:S(2)}) %collective-permute-start.10) | collective-permute-done | bytes 4128 | tf_op jit(solution)/shard_map/ppermute | solution.py:20
  94.1 7.4 %shard_map.71 = (f32[1,2048]{1,0:T(1,128)}, f32[1,1024]{1,0:T(1,128)}) custom-call(f32[1024,2048]{1,0:T(8,128)} %convolution_multiply_fusion.refs_0_.zo_ref, f32[1024,1024]{1,0:T(8,128)} %multiply_bitcast_fusion.refs_0_.ze_ref.refs_1_, f32[1024,1]{1,0:T(8,128)} %copy.14.f_ref), custom_call_target="tpu_custom_call" | custom-call | tf_op jit(solution)/shard_map/pallas_call | solution.py:61
  104.2 5.5 %collective-permute-done.12 = f32[1024]{0:T(1024)S(1)} collective-permute-done((f32[1024]{0:T(1024)S(1)}, f32[1024]{0:T(1024)S(1)}, u32[]{:S(2)}, u32[]{:S(2)}) %collective-permute-start.12) | collective-permute-done | bytes 4128 | tf_op jit(solution)/shard_map/ppermute | solution.py:20
  113.1 5.3 %collective-permute-done.15 = f32[1024]{0:T(1024)S(1)} collective-permute-done((f32[1024]{0:T(1024)S(1)}, f32[1024]{0:T(1024)S(1)}, u32[]{:S(2)}, u32[]{:S(2)}) %collective-permute-start.15) | collective-permute-done | bytes 4128 | tf_op jit(solution)/shard_map/ppermute | solution.py:20
  119.0 7.1 %shard_map.72 = f32[1024,1]{1,0:T(8,128)} custom-call(f32[1024,2048]{1,0:T(8,128)} %convolution_multiply_fusion.refs_0_.zo_ref, f32[1024,1024]{1,0:T(8,128)} %multiply_bitcast_fusion.refs_0_.ze_ref.refs_1_, f32[1,2048]{1,0:T(1,128)} %get-tuple-element.21.refs_2_.go_ref, f32[1,1024]{1,0:T(1,128)} %bitcast.116), custom_call_target="tpu_custom_call" | custom-call | tf_op jit(solution)/shard_map/pallas_call | solution.py:40
  129.9 2.9 %collective-permute-done.17 = f32[1024]{0:T(1024)S(1)} collective-permute-done((f32[1024]{0:T(1024)S(1)}, f32[1024]{0:T(1024)S(1)}, u32[]{:S(2)}, u32[]{:S(2)}) %collective-permute-start.17) | collective-permute-done | bytes 4128 | tf_op jit(solution)/shard_map/ppermute | solution.py:20
  135.5 11.3 %shard_map.73 = f32[1024,768]{1,0:T(8,128)} custom-call(f32[1024,2048]{1,0:T(8,128)} %convolution_multiply_fusion.refs_0_.zo_ref, f32[1024,1024]{1,0:T(8,128)} %multiply_bitcast_fusion.refs_0_.ze_ref.refs_1_, f32[1,2048]{1,0:T(1,128)} %get-tuple-element.21.refs_2_.go_ref, f32[1,1024]{1,0:T(1,128)} %bitcast.117, f32[1024,1]{1,0:T(8,128)} %copy.15.l_ref, ...), custom_call_target="tpu_custom_call" | custom-call | tf_op jit(solution)/shard_map/pallas_call | solution.py:91
  146.8 2.9 %constant_dynamic-slice_fusion.2 = (f32[256,768]{1,0:T(8,128)S(1)}, f32[256,768]{1,0:T(8,128)}, f32[256,768]{1,0:T(8,128)}) fusion(f32[1024,768]{1,0:T(8,128)} %shard_map.73, s32[]{:T(128)S(6)} %select_n.287, s32[]{:T(128)S(6)} %select_n.291, s32[]{:T(128)S(6)} %select_n.289), kind=kLoop, calls=%fused_computation.70 | loop fusion | bytes 4718604 | tf_op jit(solution)/shard_map/dynamic_slice | solution.py:202
  151.7 17.9 %collective-permute-done.21 = f32[256,768]{1,0:T(8,128)S(1)} collective-permute-done((f32[256,768]{1,0:T(8,128)}, f32[256,768]{1,0:T(8,128)S(1)}, u32[]{:S(2)}, u32[]{:S(2)}) %collective-permute-start.21) | collective-permute-done | bytes 786464 | tf_op jit(solution)/shard_map/ppermute | solution.py:20
  171.4 14.9 %collective-permute-done.19 = f32[256,768]{1,0:T(8,128)} collective-permute-done((f32[256,768]{1,0:T(8,128)S(1)}, f32[256,768]{1,0:T(8,128)}, u32[]{:S(2)}, u32[]{:S(2)}) %collective-permute-start.19) | collective-permute-done | bytes 786464 | tf_op jit(solution)/shard_map/ppermute | solution.py:20
  190.2 8.2 %collective-permute-done.24 = bf16[256,768]{1,0:T(8,128)(2,1)S(1)} collective-permute-done((bf16[256,768]{1,0:T(8,128)(2,1)S(1)}, bf16[256,768]{1,0:T(8,128)(2,1)S(1)}, u32[]{:S(2)}, u32[]{:S(2)}) %collective-permute-start.24) | collective-permute-done | bytes 393248 | tf_op jit(solution)/shard_map/ppermute | solution.py:20
  200.1 9.1 %collective-permute-done.22 = bf16[256,768]{1,0:T(8,128)(2,1)S(1)} collective-permute-done((bf16[256,768]{1,0:T(8,128)(2,1)S(1)}, bf16[256,768]{1,0:T(8,128)(2,1)S(1)}, u32[]{:S(2)}, u32[]{:S(2)}) %collective-permute-start.22) | collective-permute-done | bytes 393248 | tf_op jit(solution)/shard_map/ppermute | solution.py:20
  (101 shorter events, 44.4 us)
Async XLA Ops:
  9.8 18.6 %collective-permute-start = (bf16[1024,768]{1,0:T(8,128)(2,1)}, bf16[1024,768]{1,0:T(8,128)(2,1)S(1)}, u32[]{:S(2)}, u32[]{:S(2)}) collective-permute-start(bf16[1024,768]{1,0:T(8,128)(2,1)} %get-tuple-element.17), channel_id=1, source_target_pairs={{0,4},{4,8},{8,12},{12,16},{16,20},{20,24},{24,28},{28,32},{32,36}... | collective-permute-start | bytes 4718600 | tf_op jit(solution)/shard_map/ppermute | solution.py:20
  9.8 23.5 %collective-permute-start.1 = (bf16[1024,768]{1,0:T(8,128)(2,1)}, bf16[1024,768]{1,0:T(8,128)(2,1)}, u32[]{:S(2)}, u32[]{:S(2)}) collective-permute-start(bf16[1024,768]{1,0:T(8,128)(2,1)} %get-tuple-element.16), channel_id=1, source_target_pairs={{0,124},{4,0},{8,4},{12,8},{16,12},{20,16},{24,20},{28,24},{32,28}... | collective-permute-start | bytes 4718600 | tf_op jit(solution)/shard_map/ppermute | solution.py:20
  43.8 7.2 %collective-permute-start.4 = (f32[1024]{0:T(1024)S(1)}, f32[1024]{0:T(1024)S(1)}, u32[]{:S(2)}, u32[]{:S(2)}) collective-permute-start(f32[1024]{0:T(1024)S(1)} %select_reduce_fusion), channel_id=1, source_target_pairs={{0,3},{1,0},{2,1},{3,2},{4,7},{5,4},{6,5},{7,6},{8,11},{9,8},{10,9... | collective-permute-start | bytes 12296 | tf_op jit(solution)/shard_map/ppermute | solution.py:20
  47.8 4.0 %collective-permute-start.3 = (f32[1024]{0:T(1024)S(1)}, f32[1024]{0:T(1024)S(1)}, u32[]{:S(2)}, u32[]{:S(2)}) collective-permute-start(f32[1024]{0:T(1024)S(1)} %select_reduce_fusion), channel_id=1, source_target_pairs={{0,2},{1,3},{2,0},{3,1},{4,6},{5,7},{6,4},{7,5},{8,10},{9,11},{10,... | collective-permute-start | bytes 12296 | tf_op jit(solution)/shard_map/ppermute | solution.py:20
  47.8 4.0 %collective-permute-start.2 = (f32[1024]{0:T(1024)S(1)}, f32[1024]{0:T(1024)S(1)}, u32[]{:S(2)}, u32[]{:S(2)}) collective-permute-start(f32[1024]{0:T(1024)S(1)} %select_reduce_fusion), channel_id=1, source_target_pairs={{0,1},{1,2},{2,3},{3,0},{4,5},{5,6},{6,7},{7,4},{8,9},{9,10},{10,1... | collective-permute-start | bytes 12296 | tf_op jit(solution)/shard_map/ppermute | solution.py:20
  61.5 2.1 collective-permute-start.6
  62.9 6.4 %collective-permute-start.5 = (f32[1024]{0:T(1024)S(1)}, f32[1024]{0:T(1024)S(1)}, u32[]{:S(2)}, u32[]{:S(2)}) collective-permute-start(f32[1024]{0:T(1024)S(1)} %bitcast.135), channel_id=1, source_target_pairs={{0,124},{4,0},{8,4},{12,8},{16,12},{20,16},{24,20},{28,24},{32,28}... | collective-permute-start | bytes 12296 | tf_op jit(solution)/shard_map/ppermute | solution.py:20
  72.0 1.2 collective-permute-start.7
  72.1 6.4 %collective-permute-start.8 = (f32[1024]{0:T(1024)S(1)}, f32[1024]{0:T(1024)S(1)}, u32[]{:S(2)}, u32[]{:S(2)}) collective-permute-start(f32[1024]{0:T(1024)S(1)} %bitcast.131), channel_id=1, source_target_pairs={{0,124},{4,0},{8,4},{12,8},{16,12},{20,16},{24,20},{28,24},{32,28}... | collective-permute-start | bytes 12296 | tf_op jit(solution)/shard_map/ppermute | solution.py:20
  87.4 2.5 %collective-permute-start.11 = (f32[1024]{0:T(1024)S(1)}, f32[1024]{0:T(1024)S(1)}, u32[]{:S(2)}, u32[]{:S(2)}) collective-permute-start(f32[1024]{0:T(1024)S(1)} %reduce.6), channel_id=1, source_target_pairs={{0,3},{1,0},{2,1},{3,2},{4,7},{5,4},{6,5},{7,6},{8,11},{9,8},{10,9... | collective-permute-start | bytes 12296 | tf_op jit(solution)/shard_map/ppermute | solution.py:20
  88.3 4.0 %collective-permute-start.10 = (f32[1024]{0:T(1024)S(1)}, f32[1024]{0:T(1024)S(1)}, u32[]{:S(2)}, u32[]{:S(2)}) collective-permute-start(f32[1024]{0:T(1024)S(1)} %reduce.6), channel_id=1, source_target_pairs={{0,2},{1,3},{2,0},{3,1},{4,6},{5,7},{6,4},{7,5},{8,10},{9,11},{10,... | collective-permute-start | bytes 12296 | tf_op jit(solution)/shard_map/ppermute | solution.py:20
  88.7 3.7 %collective-permute-start.9 = (f32[1024]{0:T(1024)S(1)}, f32[1024]{0:T(1024)S(1)}, u32[]{:S(2)}, u32[]{:S(2)}) collective-permute-start(f32[1024]{0:T(1024)S(1)} %reduce.6), channel_id=1, source_target_pairs={{0,1},{1,2},{2,3},{3,0},{4,5},{5,6},{6,7},{7,4},{8,9},{9,10},{10,1... | collective-permute-start | bytes 12296 | tf_op jit(solution)/shard_map/ppermute | solution.py:20
  102.2 1.9 collective-permute-start.13
  103.3 6.4 %collective-permute-start.12 = (f32[1024]{0:T(1024)S(1)}, f32[1024]{0:T(1024)S(1)}, u32[]{:S(2)}, u32[]{:S(2)}) collective-permute-start(f32[1024]{0:T(1024)S(1)} %bitcast.137), channel_id=1, source_target_pairs={{0,124},{4,0},{8,4},{12,8},{16,12},{20,16},{24,20},{28,24},{32,28}... | collective-permute-start | bytes 12296 | tf_op jit(solution)/shard_map/ppermute | solution.py:20
  112.1 6.4 %collective-permute-start.15 = (f32[1024]{0:T(1024)S(1)}, f32[1024]{0:T(1024)S(1)}, u32[]{:S(2)}, u32[]{:S(2)}) collective-permute-start(f32[1024]{0:T(1024)S(1)} %bitcast.130), channel_id=1, source_target_pairs={{0,124},{4,0},{8,4},{12,8},{16,12},{20,16},{24,20},{28,24},{32,28}... | collective-permute-start | bytes 12296 | tf_op jit(solution)/shard_map/ppermute | solution.py:20
  127.4 2.5 %collective-permute-start.18 = (f32[1024]{0:T(1024)S(1)}, f32[1024]{0:T(1024)S(1)}, u32[]{:S(2)}, u32[]{:S(2)}) collective-permute-start(f32[1024]{0:T(1024)S(1)} %reduce.9), channel_id=1, source_target_pairs={{0,3},{1,0},{2,1},{3,2},{4,7},{5,4},{6,5},{7,6},{8,11},{9,8},{10,9... | collective-permute-start | bytes 12296 | tf_op jit(solution)/shard_map/ppermute | solution.py:20
  128.9 4.0 %collective-permute-start.17 = (f32[1024]{0:T(1024)S(1)}, f32[1024]{0:T(1024)S(1)}, u32[]{:S(2)}, u32[]{:S(2)}) collective-permute-start(f32[1024]{0:T(1024)S(1)} %reduce.9), channel_id=1, source_target_pairs={{0,2},{1,3},{2,0},{3,1},{4,6},{5,7},{6,4},{7,5},{8,10},{9,11},{10,... | collective-permute-start | bytes 12296 | tf_op jit(solution)/shard_map/ppermute | solution.py:20
  129.5 3.7 %collective-permute-start.16 = (f32[1024]{0:T(1024)S(1)}, f32[1024]{0:T(1024)S(1)}, u32[]{:S(2)}, u32[]{:S(2)}) collective-permute-start(f32[1024]{0:T(1024)S(1)} %reduce.9), channel_id=1, source_target_pairs={{0,1},{1,2},{2,3},{3,0},{4,5},{5,6},{6,7},{7,4},{8,9},{9,10},{10,1... | collective-permute-start | bytes 12296 | tf_op jit(solution)/shard_map/ppermute | solution.py:20
  149.7 19.9 %collective-permute-start.21 = (f32[256,768]{1,0:T(8,128)}, f32[256,768]{1,0:T(8,128)S(1)}, u32[]{:S(2)}, u32[]{:S(2)}) collective-permute-start(f32[256,768]{1,0:T(8,128)} %get-tuple-element.14), channel_id=1, source_target_pairs={{0,3},{1,0},{2,1},{3,2},{4,7},{5,4},{6,5},{7,6},{8,11},{9,8},{10,9... | collective-permute-start | bytes 2359304 | tf_op jit(solution)/shard_map/ppermute | solution.py:20
  150.3 21.1 %collective-permute-start.20 = (f32[256,768]{1,0:T(8,128)}, f32[256,768]{1,0:T(8,128)}, u32[]{:S(2)}, u32[]{:S(2)}) collective-permute-start(f32[256,768]{1,0:T(8,128)} %get-tuple-element.15), channel_id=1, source_target_pairs={{0,2},{1,3},{2,0},{3,1},{4,6},{5,7},{6,4},{7,5},{8,10},{9,11},{10,... | collective-permute-start | bytes 2359304 | tf_op jit(solution)/shard_map/ppermute | solution.py:20
  151.2 35.1 %collective-permute-start.19 = (f32[256,768]{1,0:T(8,128)S(1)}, f32[256,768]{1,0:T(8,128)}, u32[]{:S(2)}, u32[]{:S(2)}) collective-permute-start(f32[256,768]{1,0:T(8,128)S(1)} %get-tuple-element.13), channel_id=1, source_target_pairs={{0,1},{1,2},{2,3},{3,0},{4,5},{5,6},{6,7},{7,4},{8,9},{9,10},{10,1... | collective-permute-start | bytes 2359304 | tf_op jit(solution)/shard_map/ppermute | solution.py:20
  188.0 10.3 %collective-permute-start.24 = (bf16[256,768]{1,0:T(8,128)(2,1)S(1)}, bf16[256,768]{1,0:T(8,128)(2,1)S(1)}, u32[]{:S(2)}, u32[]{:S(2)}) collective-permute-start(bf16[256,768]{1,0:T(8,128)(2,1)S(1)} %add_convert_fusion), channel_id=1, source_target_pairs={{0,3},{1,0},{2,1},{3,2},{4,7},{5,4},{6,5},{7,6},{8,11},{9,8},{10,9... | collective-permute-start | bytes 1179656 | tf_op jit(solution)/shard_map/ppermute | solution.py:20
  188.2 11.9 %collective-permute-start.23 = (bf16[256,768]{1,0:T(8,128)(2,1)S(1)}, bf16[256,768]{1,0:T(8,128)(2,1)S(1)}, u32[]{:S(2)}, u32[]{:S(2)}) collective-permute-start(bf16[256,768]{1,0:T(8,128)(2,1)S(1)} %add_convert_fusion), channel_id=1, source_target_pairs={{0,2},{1,3},{2,0},{3,1},{4,6},{5,7},{6,4},{7,5},{8,10},{9,11},{10,... | collective-permute-start | bytes 1179656 | tf_op jit(solution)/shard_map/ppermute | solution.py:20
  188.9 20.3 %collective-permute-start.22 = (bf16[256,768]{1,0:T(8,128)(2,1)S(1)}, bf16[256,768]{1,0:T(8,128)(2,1)S(1)}, u32[]{:S(2)}, u32[]{:S(2)}) collective-permute-start(bf16[256,768]{1,0:T(8,128)(2,1)S(1)} %add_convert_fusion), channel_id=1, source_target_pairs={{0,1},{1,2},{2,3},{3,0},{4,5},{5,6},{6,7},{7,4},{8,9},{9,10},{10,1... | collective-permute-start | bytes 1179656 | tf_op jit(solution)/shard_map/ppermute | solution.py:20
  (6 other events, 68.4 us)

commit v3 on v2

--- a/solution.py
+++ b/solution.py
@@ -194,17 +194,8 @@
     source_pot = epsilon * (log_src - row)
     numer = map_call(zo, ze, go, ge, row.reshape(-1, 1), targets, extra)
 
-    rows = sources.shape[0]
-    part = rows // narrow_count
-    mine_part = lax.dynamic_slice_in_dim(numer, c * part, part, 0)
-    for k in range(1, narrow_count):
-        dest = (c + k) % narrow_count
-        piece = lax.dynamic_slice_in_dim(numer, dest * part, part, 0)
-        mine_part = mine_part + shifted(piece, "narrow", k)
-    done = mine_part.astype(jnp.bfloat16)
-    pieces = jnp.stack([done] + [shifted(done, "narrow", k) for k in range(1, narrow_count)])
-    order = (c - jnp.arange(narrow_count, dtype=jnp.int32)) % narrow_count
-    mapped = pieces[order].reshape(rows, feature_count)
+    summed = lax.psum_scatter(numer, "narrow", scatter_dimension=0, tiled=True)
+    mapped = lax.all_gather(summed.astype(jnp.bfloat16), "narrow", axis=0, tiled=True)
     return (source_pot, g_own, mapped)
 
 

time: 212 us -> 240 us (1.13)
  starting transfers between devices: 16.2 us -> 30.5 us
  between operations: 10.5 us -> 23.8 us
    ppermute x25 -> x19, waiting for transfers between devices: 90.6 us -> 28.3 us  [shifted(): return lax.ppermute(x, axis, route)]
    reduce_scatter x0 -> x1, waiting for transfers between devices: none -> 36.7 us  [shards(): summed = lax.psum_scatter(numer, 'narrow', scatter_dimension=0, tiled=True)]
    all_gather x0 -> x1, waiting for transfers between devices: none -> 25.8 us  [shards(): lax.all_gather(summed.astype(jnp.bfloat16), 'narrow', axis=0, tiled=True)]
    ppermute x25 -> x19, starting transfers between devices: 16.2 us -> 30.5 us  [shifted(): return lax.ppermute(x, axis, route)]
    dynamic_slice x1 -> x0, local copies, waits for them, and re-layouts: 2.88 us -> none  [shards(): piece = lax.dynamic_slice_in_dim(numer, dest * part, part, 0)]
    unnamed x14 -> x15, local copies, waits for them, and re-layouts: 0.07 us -> 2.72 us
  transfers between devices with their start and end apart: 25 -> 21, of which waited for: 22 -> 18; matrix products, arithmetic and copies ran while one was open for 5% -> 4% of each run, Pallas kernels for 3% -> 2%
where the time goes in v3:
time: 240 us; the launch traced here: 237 us
  waiting for transfers between devices  90.8 us (38%)
  Pallas kernels  50.7 us (21%)
  starting transfers between devices  30.5 us (13%)
  between operations  23.8 us (10%)
  local copies, waits for them, and re-layouts  15.4 us (6%)
  other arithmetic  14.4 us (6%)
  matrix products  11.3 us (5%)
    reduce_scatter x1, waiting for transfers between devices, shards(): summed = lax.psum_scatter(numer, 'narrow', scatter_dimension=0, tiled=True)  36.7 us
    ppermute x19, starting transfers between devices, shifted(): return lax.ppermute(x, axis, route)  30.5 us
    ppermute x19, waiting for transfers between devices, shifted(): return lax.ppermute(x, axis, route)  28.3 us
    all_gather x1, waiting for transfers between devices, shards(): lax.all_gather(summed.astype(jnp.bfloat16), 'narrow', axis=0, tiled=True)  25.8 us
    pallas_call x4, Pallas kernels, row_lse_call(): pl.pallas_call(_row_kernel, grid=(rows // tm,), in_specs=in_specs, out_sp...  24.5 us
    pallas_call x2, Pallas kernels, col_lse_call(): pl.pallas_call(_col_kernel, grid=(steps,), in_specs=[pl.BlockSpec((rows,...  14.8 us
    pallas_call x1, Pallas kernels, map_call(): pl.pallas_call(_map_kernel, grid=(rows // tm,), in_specs=[pl.BlockSpec((t...  11.4 us
    dot_general x1, matrix products, shards(): lax.dot_general(sources, targets, (((1,), (1,)), ((), ())), preferred_ele...  7.56 us
  transfers between devices with their start and end apart: 21, of which 18 were waited for; matrix products, arithmetic and copies ran while one was open for 4% of the time, Pallas kernels for 2%

profile of v3, /device:TPU:121, one launch (start us, length us, event | category | flops | bytes accessed | tf_op | source)
XLA Modules:
  0.0 237.0 jit_solution(1991231013289990696)
XLA Ops:
  12.4 3.9 %dynamic-slice_bitcast_fusion = (bf16[1024,768]{1,0:T(8,128)(2,1)}, bf16[1024,768]{1,0:T(8,128)(2,1)}) fusion(bf16[2,1024,768]{2,1,0:T(8,128)(2,1)} %bitcast.105, s32[]{:T(128)S(6)} %select_n.232, s32[]{:T(128)S(6)} %select_n.229), kind=kLoop, calls=%fused_computation.5 | loop fusion | bytes 6291464 | tf_op jit(solution)/shard_map/squeeze | solution.py:145
  16.9 4.5 %collective-permute-start = (bf16[1024,768]{1,0:T(8,128)(2,1)}, bf16[1024,768]{1,0:T(8,128)(2,1)}, u32[]{:S(2)}, u32[]{:S(2)}) collective-permute-start(bf16[1024,768]{1,0:T(8,128)(2,1)} %get-tuple-element.14), channel_id=1, source_target_pairs={{0,4},{4,8},{8,12},{12,16},{16,20},{20,24},{24,28},{28,32},{32,36}... | collective-permute-start | bytes 4718600 | tf_op jit(solution)/shard_map/ppermute | solution.py:20
  25.3 7.6 %convolution_multiply_fusion.refs_0_.zo_ref = f32[1024,2048]{1,0:T(8,128)} fusion(bf16[1024,768]{1,0:T(8,128)(2,1)S(1)} %copy-done, bf16[2048,768]{1,0:T(8,128)(2,1)} %to_ref.1), kind=kOutput, calls=%fused_computation.3 | convolution fusion | flops 3223322624 | bytes 13107200 | tf_op jit(solution)/shard_map/dot_general | solution.py:149
  33.5 5.8 %shard_map.67 = f32[1024,1]{1,0:T(8,128)} custom-call(f32[1024,2048]{1,0:T(8,128)} %convolution_multiply_fusion.refs_0_.zo_ref, f32[1,2048]{1,0:T(1,128)} %reshape.302.refs_1_), custom_call_target="tpu_custom_call" | custom-call | tf_op jit(solution)/shard_map/pallas_call | solution.py:40
  41.3 3.8 %multiply_bitcast_fusion.refs_0_.ze_ref.refs_1_ = f32[1024,1024]{1,0:T(8,128)} fusion(bf16[1024,768]{1,0:T(8,128)(2,1)S(1)} %broadcast_select_fusion.te_ref, bf16[1024,768]{1,0:T(8,128)(2,1)S(1)} %copy-done), kind=kOutput, calls=%fused_computation.4 | convolution fusion | flops 1611661312 | bytes 7340032 | tf_op jit(solution)/shard_map/dot_general | solution.py:153
  45.6 4.5 %shard_map.68 = f32[1024,1]{1,0:T(8,128)} custom-call(f32[1024,1024]{1,0:T(8,128)} %multiply_bitcast_fusion.refs_0_.ze_ref.refs_1_, f32[1,1024]{1,0:T(1,128)} %reshape.303.refs_1_), custom_call_target="tpu_custom_call" | custom-call | tf_op jit(solution)/shard_map/pallas_call | solution.py:40
  51.6 2.4 %collective-permute-start.4 = (f32[1024]{0:T(1024)S(1)}, f32[1024]{0:T(1024)S(1)}, u32[]{:S(2)}, u32[]{:S(2)}) collective-permute-start(f32[1024]{0:T(1024)S(1)} %select_reduce_fusion), channel_id=1, source_target_pairs={{0,3},{1,0},{2,1},{3,2},{4,7},{5,4},{6,5},{7,6},{8,11},{9,8},{10,9... | collective-permute-start | bytes 12296 | tf_op jit(solution)/shard_map/ppermute | solution.py:20
  60.1 7.4 %shard_map.69 = (f32[1,2048]{1,0:T(1,128)}, f32[1,1024]{1,0:T(1,128)}) custom-call(f32[1024,2048]{1,0:T(8,128)} %convolution_multiply_fusion.refs_0_.zo_ref, f32[1024,1024]{1,0:T(8,128)} %multiply_bitcast_fusion.refs_0_.ze_ref.refs_1_, f32[1024,1]{1,0:T(8,128)} %copy.13.f_ref), custom_call_target="tpu_custom_call" | custom-call | tf_op jit(solution)/shard_map/pallas_call | solution.py:61
  67.5 7.6 %collective-permute-start.6 = (f32[1024]{0:T(1024)S(1)}, f32[1024]{0:T(1024)S(1)}, u32[]{:S(2)}, u32[]{:S(2)}) collective-permute-start(f32[1024]{0:T(1024)S(1)} %bitcast.124), channel_id=1, source_target_pairs={{0,4},{4,8},{8,12},{12,16},{16,20},{20,24},{24,28},{28,32},{32,36}... | collective-permute-start | bytes 12296 | tf_op jit(solution)/shard_map/ppermute | solution.py:20
  75.9 5.5 %collective-permute-done.5 = f32[1024]{0:T(1024)S(1)} collective-permute-done((f32[1024]{0:T(1024)S(1)}, f32[1024]{0:T(1024)S(1)}, u32[]{:S(2)}, u32[]{:S(2)}) %collective-permute-start.5) | collective-permute-done | bytes 4128 | tf_op jit(solution)/shard_map/ppermute | solution.py:20
  82.0 1.9 fusion.24
  85.3 5.3 %collective-permute-done.8 = f32[1024]{0:T(1024)S(1)} collective-permute-done((f32[1024]{0:T(1024)S(1)}, f32[1024]{0:T(1024)S(1)}, u32[]{:S(2)}, u32[]{:S(2)}) %collective-permute-start.8) | collective-permute-done | bytes 4128 | tf_op jit(solution)/shard_map/ppermute | solution.py:20
  91.2 7.1 %shard_map.70 = f32[1024,1]{1,0:T(8,128)} custom-call(f32[1024,2048]{1,0:T(8,128)} %convolution_multiply_fusion.refs_0_.zo_ref, f32[1024,1024]{1,0:T(8,128)} %multiply_bitcast_fusion.refs_0_.ze_ref.refs_1_, f32[1,2048]{1,0:T(1,128)} %get-tuple-element.22.refs_2_, f32[1,1024]{1,0:T(1,128)} %bitcast.115), custom_call_target="tpu_custom_call" | custom-call | tf_op jit(solution)/shard_map/pallas_call | solution.py:40
  106.2 7.4 %shard_map.71 = (f32[1,2048]{1,0:T(1,128)}, f32[1,1024]{1,0:T(1,128)}) custom-call(f32[1024,2048]{1,0:T(8,128)} %convolution_multiply_fusion.refs_0_.zo_ref, f32[1024,1024]{1,0:T(8,128)} %multiply_bitcast_fusion.refs_0_.ze_ref.refs_1_, f32[1024,1]{1,0:T(8,128)} %copy.14.f_ref), custom_call_target="tpu_custom_call" | custom-call | tf_op jit(solution)/shard_map/pallas_call | solution.py:61
  113.7 5.1 %collective-permute-start.13 = (f32[1024]{0:T(1024)S(1)}, f32[1024]{0:T(1024)S(1)}, u32[]{:S(2)}, u32[]{:S(2)}) collective-permute-start(f32[1024]{0:T(1024)S(1)} %bitcast.127), channel_id=1, source_target_pairs={{0,4},{4,8},{8,12},{12,16},{16,20},{20,24},{24,28},{28,32},{32,36}... | collective-permute-start | bytes 12296 | tf_op jit(solution)/shard_map/ppermute | solution.py:20
  122.2 5.0 %collective-permute-start.14 = (f32[1024]{0:T(1024)S(1)}, f32[1024]{0:T(1024)S(1)}, u32[]{:S(2)}, u32[]{:S(2)}) collective-permute-start(f32[1024]{0:T(1024)S(1)} %bitcast.122), channel_id=1, source_target_pairs={{0,4},{4,8},{8,12},{12,16},{16,20},{20,24},{24,28},{28,32},{32,36}... | collective-permute-start | bytes 12296 | tf_op jit(solution)/shard_map/ppermute | solution.py:20
  128.0 5.6 %collective-permute-done.15 = f32[1024]{0:T(1024)S(1)} collective-permute-done((f32[1024]{0:T(1024)S(1)}, f32[1024]{0:T(1024)S(1)}, u32[]{:S(2)}, u32[]{:S(2)}) %collective-permute-start.15) | collective-permute-done | bytes 4128 | tf_op jit(solution)/shard_map/ppermute | solution.py:20
  134.2 7.1 %shard_map.72 = f32[1024,1]{1,0:T(8,128)} custom-call(f32[1024,2048]{1,0:T(8,128)} %convolution_multiply_fusion.refs_0_.zo_ref, f32[1024,1024]{1,0:T(8,128)} %multiply_bitcast_fusion.refs_0_.ze_ref.refs_1_, f32[1,2048]{1,0:T(1,128)} %get-tuple-element.18.refs_2_.go_ref, f32[1,1024]{1,0:T(1,128)} %bitcast.106), custom_call_target="tpu_custom_call" | custom-call | tf_op jit(solution)/shard_map/pallas_call | solution.py:40
  145.1 3.0 %collective-permute-done.17 = f32[1024]{0:T(1024)S(1)} collective-permute-done((f32[1024]{0:T(1024)S(1)}, f32[1024]{0:T(1024)S(1)}, u32[]{:S(2)}, u32[]{:S(2)}) %collective-permute-start.17) | collective-permute-done | bytes 4128 | tf_op jit(solution)/shard_map/ppermute | solution.py:20
  151.0 11.4 %shard_map.73 = f32[1024,768]{1,0:T(8,128)} custom-call(f32[1024,2048]{1,0:T(8,128)} %convolution_multiply_fusion.refs_0_.zo_ref, f32[1024,1024]{1,0:T(8,128)} %multiply_bitcast_fusion.refs_0_.ze_ref.refs_1_, f32[1,2048]{1,0:T(1,128)} %get-tuple-element.18.refs_2_.go_ref, f32[1,1024]{1,0:T(1,128)} %bitcast.107, f32[1024,1]{1,0:T(8,128)} %copy.15.l_ref, ...), custom_call_target="tpu_custom_call" | custom-call | tf_op jit(solution)/shard_map/pallas_call | solution.py:91
  162.4 36.7 %reduce-scatter.2.cloned.1.call-done = f32[256,768]{1,0:T(8,128)} async-done(((f32[1024,768]{1,0:T(8,128)}), f32[256,768]{1,0:T(8,128)}) %reduce-scatter.2.cloned.1.call-update) | async-done | bytes 786448 | tf_op jit(solution)/shard_map/reduce_scatter | solution.py:197
  199.1 1.9 convert_element_type.3
  201.7 25.8 %all-gather.2.cloned.1.call-done = bf16[1024,768]{1,0:T(8,128)(2,1)} async-done(((bf16[256,768]{1,0:T(8,128)(2,1)}), bf16[1024,768]{1,0:T(8,128)(2,1)}) %all-gather.2.cloned.1.call-update) | async-done | bytes 1572880 | tf_op jit(solution)/shard_map/all_gather | solution.py:198
  227.5 2.7 %copy.26 = bf16[1024,768]{1,0:T(8,128)(2,1)} copy(bf16[1024,768]{1,0:T(8,128)(2,1)} %all-gather.2.cloned.1.call-done) | data formatting | bytes 3145728
  (93 shorter events, 34.3 us)
Async XLA Ops:
  7.2 18.1 %copy-start = (bf16[1024,768]{1,0:T(8,128)(2,1)S(1)}, bf16[1024,768]{1,0:T(8,128)(2,1)}, u32[]{:S(2)}) copy-start(bf16[1024,768]{1,0:T(8,128)(2,1)} %param.4) | copy-start | bytes 4718596
  7.2 192.0 %reduce-scatter.2.cloned.1.call-start = ((), (), s32[]{:S(2)}) async-start(), calls=%async_computation.1 | async-start | bytes 3932160 | tf_op jit(solution)/shard_map/reduce_scatter | solution.py:197
  12.4 11.6 %copy-start.4 = (s32[32]{0:T(128)S(1)}, s32[32]{0:T(128)}, u32[]{:S(2)}) copy-start(s32[32]{0:T(128)} %param.7) | copy-start | bytes 388
  16.3 23.4 %collective-permute-start.1 = (bf16[1024,768]{1,0:T(8,128)(2,1)}, bf16[1024,768]{1,0:T(8,128)(2,1)S(1)}, u32[]{:S(2)}, u32[]{:S(2)}) collective-permute-start(bf16[1024,768]{1,0:T(8,128)(2,1)} %get-tuple-element.13), channel_id=1, source_target_pairs={{0,124},{4,0},{8,4},{12,8},{16,12},{20,16},{24,20},{28,24},{32,28}... | collective-permute-start | bytes 4718600 | tf_op jit(solution)/shard_map/ppermute | solution.py:20
  16.9 22.8 %collective-permute-start = (bf16[1024,768]{1,0:T(8,128)(2,1)}, bf16[1024,768]{1,0:T(8,128)(2,1)}, u32[]{:S(2)}, u32[]{:S(2)}) collective-permute-start(bf16[1024,768]{1,0:T(8,128)(2,1)} %get-tuple-element.14), channel_id=1, source_target_pairs={{0,4},{4,8},{8,12},{12,16},{16,20},{20,24},{24,28},{28,32},{32,36}... | collective-permute-start | bytes 4718600 | tf_op jit(solution)/shard_map/ppermute | solution.py:20
  51.6 5.7 %collective-permute-start.4 = (f32[1024]{0:T(1024)S(1)}, f32[1024]{0:T(1024)S(1)}, u32[]{:S(2)}, u32[]{:S(2)}) collective-permute-start(f32[1024]{0:T(1024)S(1)} %select_reduce_fusion), channel_id=1, source_target_pairs={{0,3},{1,0},{2,1},{3,2},{4,7},{5,4},{6,5},{7,6},{8,11},{9,8},{10,9... | collective-permute-start | bytes 12296 | tf_op jit(solution)/shard_map/ppermute | solution.py:20
  54.1 4.0 %collective-permute-start.3 = (f32[1024]{0:T(1024)S(1)}, f32[1024]{0:T(1024)S(1)}, u32[]{:S(2)}, u32[]{:S(2)}) collective-permute-start(f32[1024]{0:T(1024)S(1)} %select_reduce_fusion), channel_id=1, source_target_pairs={{0,2},{1,3},{2,0},{3,1},{4,6},{5,7},{6,4},{7,5},{8,10},{9,11},{10,... | collective-permute-start | bytes 12296 | tf_op jit(solution)/shard_map/ppermute | solution.py:20
  54.7 3.7 %collective-permute-start.2 = (f32[1024]{0:T(1024)S(1)}, f32[1024]{0:T(1024)S(1)}, u32[]{:S(2)}, u32[]{:S(2)}) collective-permute-start(f32[1024]{0:T(1024)S(1)} %select_reduce_fusion), channel_id=1, source_target_pairs={{0,1},{1,2},{2,3},{3,0},{4,5},{5,6},{6,7},{7,4},{8,9},{9,10},{10,1... | collective-permute-start | bytes 12296 | tf_op jit(solution)/shard_map/ppermute | solution.py:20
  67.5 8.3 %collective-permute-start.6 = (f32[1024]{0:T(1024)S(1)}, f32[1024]{0:T(1024)S(1)}, u32[]{:S(2)}, u32[]{:S(2)}) collective-permute-start(f32[1024]{0:T(1024)S(1)} %bitcast.124), channel_id=1, source_target_pairs={{0,4},{4,8},{8,12},{12,16},{16,20},{20,24},{24,28},{28,32},{32,36}... | collective-permute-start | bytes 12296 | tf_op jit(solution)/shard_map/ppermute | solution.py:20
  75.0 6.4 %collective-permute-start.5 = (f32[1024]{0:T(1024)S(1)}, f32[1024]{0:T(1024)S(1)}, u32[]{:S(2)}, u32[]{:S(2)}) collective-permute-start(f32[1024]{0:T(1024)S(1)} %bitcast.125), channel_id=1, source_target_pairs={{0,124},{4,0},{8,4},{12,8},{16,12},{20,16},{24,20},{28,24},{32,28}... | collective-permute-start | bytes 12296 | tf_op jit(solution)/shard_map/ppermute | solution.py:20
  84.0 1.2 collective-permute-start.7
  84.2 6.4 %collective-permute-start.8 = (f32[1024]{0:T(1024)S(1)}, f32[1024]{0:T(1024)S(1)}, u32[]{:S(2)}, u32[]{:S(2)}) collective-permute-start(f32[1024]{0:T(1024)S(1)} %bitcast.121), channel_id=1, source_target_pairs={{0,124},{4,0},{8,4},{12,8},{16,12},{20,16},{24,20},{28,24},{32,28}... | collective-permute-start | bytes 12296 | tf_op jit(solution)/shard_map/ppermute | solution.py:20
  99.5 2.5 %collective-permute-start.11 = (f32[1024]{0:T(1024)S(1)}, f32[1024]{0:T(1024)S(1)}, u32[]{:S(2)}, u32[]{:S(2)}) collective-permute-start(f32[1024]{0:T(1024)S(1)} %reduce.6), channel_id=1, source_target_pairs={{0,3},{1,0},{2,1},{3,2},{4,7},{5,4},{6,5},{7,6},{8,11},{9,8},{10,9... | collective-permute-start | bytes 12296 | tf_op jit(solution)/shard_map/ppermute | solution.py:20
  99.7 4.0 %collective-permute-start.10 = (f32[1024]{0:T(1024)S(1)}, f32[1024]{0:T(1024)S(1)}, u32[]{:S(2)}, u32[]{:S(2)}) collective-permute-start(f32[1024]{0:T(1024)S(1)} %reduce.6), channel_id=1, source_target_pairs={{0,2},{1,3},{2,0},{3,1},{4,6},{5,7},{6,4},{7,5},{8,10},{9,11},{10,... | collective-permute-start | bytes 12296 | tf_op jit(solution)/shard_map/ppermute | solution.py:20
  99.7 4.7 %collective-permute-start.9 = (f32[1024]{0:T(1024)S(1)}, f32[1024]{0:T(1024)S(1)}, u32[]{:S(2)}, u32[]{:S(2)}) collective-permute-start(f32[1024]{0:T(1024)S(1)} %reduce.6), channel_id=1, source_target_pairs={{0,1},{1,2},{2,3},{3,0},{4,5},{5,6},{6,7},{7,4},{8,9},{9,10},{10,1... | collective-permute-start | bytes 12296 | tf_op jit(solution)/shard_map/ppermute | solution.py:20
  113.6 6.4 %collective-permute-start.12 = (f32[1024]{0:T(1024)S(1)}, f32[1024]{0:T(1024)S(1)}, u32[]{:S(2)}, u32[]{:S(2)}) collective-permute-start(f32[1024]{0:T(1024)S(1)} %bitcast.126), channel_id=1, source_target_pairs={{0,124},{4,0},{8,4},{12,8},{16,12},{20,16},{24,20},{28,24},{32,28}... | collective-permute-start | bytes 12296 | tf_op jit(solution)/shard_map/ppermute | solution.py:20
  113.7 6.4 %collective-permute-start.13 = (f32[1024]{0:T(1024)S(1)}, f32[1024]{0:T(1024)S(1)}, u32[]{:S(2)}, u32[]{:S(2)}) collective-permute-start(f32[1024]{0:T(1024)S(1)} %bitcast.127), channel_id=1, source_target_pairs={{0,4},{4,8},{8,12},{12,16},{16,20},{20,24},{24,28},{28,32},{32,36}... | collective-permute-start | bytes 12296 | tf_op jit(solution)/shard_map/ppermute | solution.py:20
  122.2 5.8 %collective-permute-start.14 = (f32[1024]{0:T(1024)S(1)}, f32[1024]{0:T(1024)S(1)}, u32[]{:S(2)}, u32[]{:S(2)}) collective-permute-start(f32[1024]{0:T(1024)S(1)} %bitcast.122), channel_id=1, source_target_pairs={{0,4},{4,8},{8,12},{12,16},{16,20},{20,24},{24,28},{28,32},{32,36}... | collective-permute-start | bytes 12296 | tf_op jit(solution)/shard_map/ppermute | solution.py:20
  127.3 6.4 %collective-permute-start.15 = (f32[1024]{0:T(1024)S(1)}, f32[1024]{0:T(1024)S(1)}, u32[]{:S(2)}, u32[]{:S(2)}) collective-permute-start(f32[1024]{0:T(1024)S(1)} %bitcast.120), channel_id=1, source_target_pairs={{0,124},{4,0},{8,4},{12,8},{16,12},{20,16},{24,20},{28,24},{32,28}... | collective-permute-start | bytes 12296 | tf_op jit(solution)/shard_map/ppermute | solution.py:20
  142.6 2.5 %collective-permute-start.18 = (f32[1024]{0:T(1024)S(1)}, f32[1024]{0:T(1024)S(1)}, u32[]{:S(2)}, u32[]{:S(2)}) collective-permute-start(f32[1024]{0:T(1024)S(1)} %reduce.9), channel_id=1, source_target_pairs={{0,3},{1,0},{2,1},{3,2},{4,7},{5,4},{6,5},{7,6},{8,11},{9,8},{10,9... | collective-permute-start | bytes 12296 | tf_op jit(solution)/shard_map/ppermute | solution.py:20
  144.1 4.0 %collective-permute-start.17 = (f32[1024]{0:T(1024)S(1)}, f32[1024]{0:T(1024)S(1)}, u32[]{:S(2)}, u32[]{:S(2)}) collective-permute-start(f32[1024]{0:T(1024)S(1)} %reduce.9), channel_id=1, source_target_pairs={{0,2},{1,3},{2,0},{3,1},{4,6},{5,7},{6,4},{7,5},{8,10},{9,11},{10,... | collective-permute-start | bytes 12296 | tf_op jit(solution)/shard_map/ppermute | solution.py:20
  145.0 3.7 %collective-permute-start.16 = (f32[1024]{0:T(1024)S(1)}, f32[1024]{0:T(1024)S(1)}, u32[]{:S(2)}, u32[]{:S(2)}) collective-permute-start(f32[1024]{0:T(1024)S(1)} %reduce.9), channel_id=1, source_target_pairs={{0,1},{1,2},{2,3},{3,0},{4,5},{5,6},{6,7},{7,4},{8,9},{9,10},{10,1... | collective-permute-start | bytes 12296 | tf_op jit(solution)/shard_map/ppermute | solution.py:20
  162.4 38.7 %copy-start.3 = (f32[1,2048]{1,0:T(1,128)S(1)}, f32[1,2048]{1,0:T(1,128)}, u32[]{:S(2)}) copy-start(f32[1,2048]{1,0:T(1,128)} %get-tuple-element.9) | copy-start | bytes 24580
  162.4 65.1 %all-gather.2.cloned.1.call-start = ((), (), s32[]{:S(2)}) async-start(), calls=%async_computation.2 | async-start | bytes 1966080 | tf_op jit(solution)/shard_map/all_gather | solution.py:198
  (2 other events, 8.3 us)
Sparse Core Ops, SparseCore 0:
  162.5 36.6 reduce-scatter.1
  201.4 26.0 all-gather.1

commit v4 on v3

--- a/solution.py
+++ b/solution.py
@@ -139,6 +139,10 @@
     want_right_live = (pair_count[right] > slot) & ((want_right // group_blocks) == w)
     want_left = pair_target[left, slot]
     want_left_live = (pair_count[left] > slot) & ((want_left // group_blocks) == w)
+    left2 = (w - 2 + 2 * wide_count) % wide_count
+    right2 = (w + 2) % wide_count
+    far_left_same = (pair_count[left2] > slot) & (pair_target[left2, slot] == mine)
+    far_right_same = (pair_count[right2] > slot) & (pair_target[right2, slot] == mine)
 
     blocks = targets.reshape(tgt_blocks, BLK, feature_count)
     to_right = blocks[want_right % tgt_blocks]
@@ -175,27 +179,58 @@
         own_cols, extra_cols = col_lse_call(zo, ze, (f * inv_eps).reshape(-1, 1))
         own_cols = own_cols.reshape(tgt_blocks, BLK)
         extra_cols = jnp.where(mine_live, extra_cols.reshape(-1), sentinel)
-        back_from_right = shifted(extra_cols, "wide", -1)
-        back_from_left = shifted(extra_cols, "wide", 1)
+        part_from_left = shifted(extra_cols, "wide", 1)
+        part_from_right = shifted(extra_cols, "wide", -1)
+        part_from_left2 = shifted(extra_cols, "wide", 2)
+        part_from_right2 = shifted(extra_cols, "wide", -2)
+        cover_from_left = shifted(own_cols[want_right % tgt_blocks], "wide", 1)
+        cover_from_right = shifted(own_cols[want_left % tgt_blocks], "wide", -1)
         ids = jnp.arange(tgt_blocks, dtype=jnp.int32)[:, None]
-        add_right = jnp.where(want_right_live & (ids == want_right % tgt_blocks), back_from_right[None, :], sentinel)
-        add_left = jnp.where(want_left_live & (ids == want_left % tgt_blocks), back_from_left[None, :], sentinel)
+        add_right = jnp.where(want_right_live & (ids == want_right % tgt_blocks), part_from_right[None, :], sentinel)
+        add_left = jnp.where(want_left_live & (ids == want_left % tgt_blocks), part_from_left[None, :], sentinel)
         top = jnp.maximum(own_cols, jnp.maximum(add_right, add_left))
         total = jnp.exp(own_cols - top) + jnp.exp(add_right - top) + jnp.exp(add_left - top)
-        col = top + jnp.log(total)
-        g_blocks = epsilon * (log_tgt - col)
+        g_blocks = epsilon * (log_tgt - (top + jnp.log(total)))
         g_own = g_blocks.reshape(-1)
-        send_right = g_blocks[want_right % tgt_blocks]
-        send_left = g_blocks[want_left % tgt_blocks]
-        g_extra = jnp.where(mine_from_left, shifted(send_right, "wide", 1), shifted(send_left, "wide", -1))
+        cover_e = jnp.where(mine_from_left, cover_from_left, cover_from_right)
+        other = jnp.where(mine_from_left, part_from_left2, part_from_right2)
+        other_live = jnp.where(mine_from_left, far_left_same, far_right_same)
+        other = jnp.where(other_live, other, sentinel)
+        first = jnp.where(mine_from_left, extra_cols, other)
+        second = jnp.where(mine_from_left, other, extra_cols)
+        top_e = jnp.maximum(cover_e, jnp.maximum(first, second))
+        total_e = jnp.exp(cover_e - top_e) + jnp.exp(first - top_e) + jnp.exp(second - top_e)
+        g_extra = epsilon * (log_tgt - (top_e + jnp.log(total_e)))
 
     go, ge = scaled(g_own, g_extra)
     row = narrow_lse(row_lse_call([zo, ze], [go, ge]).reshape(-1), c, narrow_count)
     source_pot = epsilon * (log_src - row)
     numer = map_call(zo, ze, go, ge, row.reshape(-1, 1), targets, extra)
 
-    summed = lax.psum_scatter(numer, "narrow", scatter_dimension=0, tiled=True)
-    mapped = lax.all_gather(summed.astype(jnp.bfloat16), "narrow", axis=0, tiled=True)
+    rows = sources.shape[0]
+    quarter = rows // narrow_count
+    half = quarter // 2
+    chunks = numer.reshape(narrow_count, 2, half, feature_count)
+
+    def chunk(index, side):
+        return lax.dynamic_index_in_dim(chunks, index % narrow_count, 0, False)[side]
+
+    far_a = shifted(chunk(c + 2, 0), "narrow", 1)
+    far_b = shifted(chunk(c + 2, 1), "narrow", -1)
+    to_right = jnp.stack([chunk(c + 1, 0) + far_a, chunk(c + 1, 1)])
+    to_left = jnp.stack([chunk(c - 1, 0), chunk(c - 1, 1) + far_b])
+    got_left = shifted(to_right, "narrow", 1)
+    got_right = shifted(to_left, "narrow", -1)
+    mine_sum = jnp.stack([chunk(c, 0), chunk(c, 1)]) + got_left + got_right
+    done = mine_sum.astype(jnp.bfloat16).reshape(quarter, feature_count)
+    q_left = shifted(done, "narrow", 1)
+    q_right = shifted(done, "narrow", -1)
+    far_half_a = shifted(q_left[:half], "narrow", 1)
+    far_half_b = shifted(q_right[half:], "narrow", -1)
+    q_far = jnp.concatenate([far_half_a, far_half_b])
+    pieces = jnp.stack([done, q_left, q_far, q_right])
+    order = (c - jnp.arange(narrow_count, dtype=jnp.int32)) % narrow_count
+    mapped = pieces[order].reshape(rows, feature_count)
     return (source_pot, g_own, mapped)
 
 

time: 240 us -> 217 us (0.904)
  waiting for transfers between devices: 90.8 us -> 72.4 us
  between operations: 23.8 us -> 14.8 us
  starting transfers between devices: 30.5 us -> 37.1 us
    ppermute x19 -> x31, waiting for transfers between devices: 28.3 us -> 72.4 us  [shifted(): return lax.ppermute(x, axis, route)]
    reduce_scatter x1 -> x0, waiting for transfers between devices: 36.7 us -> none  [shards(): summed = lax.psum_scatter(numer, 'narrow', scatter_dimension=0, tiled=True)]
    all_gather x1 -> x0, waiting for transfers between devices: 25.8 us -> none  [shards(): lax.all_gather(summed.astype(jnp.bfloat16), 'narrow', axis=0, tiled=True)]
    ppermute x19 -> x31, starting transfers between devices: 30.5 us -> 37.1 us  [shifted(): return lax.ppermute(x, axis, route)]
    unnamed x15 -> x14, local copies, waits for them, and re-layouts: 2.72 us -> 0.07 us
  transfers between devices with their start and end apart: 21 -> 31, of which waited for: 18 -> 21; matrix products, arithmetic and copies ran while one was open for 4% -> 7% of each run, Pallas kernels for 2% -> 3%
where the time goes in v4:
time: 217 us; the launch traced here: 216 us
  waiting for transfers between devices  72.4 us (33%)
  Pallas kernels  50.7 us (23%)
  starting transfers between devices  37.1 us (17%)
  local copies, waits for them, and re-layouts  16.4 us (8%)
  between operations  14.8 us (7%)
  other arithmetic  12.7 us (6%)
  matrix products  11.3 us (5%)
    ppermute x31, waiting for transfers between devices, shifted(): return lax.ppermute(x, axis, route)  72.4 us
    ppermute x31, starting transfers between devices, shifted(): return lax.ppermute(x, axis, route)  37.1 us
    pallas_call x4, Pallas kernels, row_lse_call(): pl.pallas_call(_row_kernel, grid=(rows // tm,), in_specs=in_specs, out_sp...  24.5 us
    pallas_call x2, Pallas kernels, col_lse_call(): pl.pallas_call(_col_kernel, grid=(steps,), in_specs=[pl.BlockSpec((rows,...  14.8 us
    pallas_call x1, Pallas kernels, map_call(): pl.pallas_call(_map_kernel, grid=(rows // tm,), in_specs=[pl.BlockSpec((t...  11.4 us
    dot_general x1, matrix products, shards(): lax.dot_general(sources, targets, (((1,), (1,)), ((), ())), preferred_ele...  7.55 us
  transfers between devices with their start and end apart: 31, of which 21 were waited for; matrix products, arithmetic and copies ran while one was open for 7% of the time, Pallas kernels for 3%

profile of v4, /device:TPU:121, one launch (start us, length us, event | category | flops | bytes accessed | tf_op | source)
XLA Modules:
  0.0 215.5 jit_solution(8025731993944991690)
XLA Ops:
  6.1 3.8 %dynamic-slice_bitcast_fusion = (bf16[1024,768]{1,0:T(8,128)(2,1)}, bf16[1024,768]{1,0:T(8,128)(2,1)}) fusion(bf16[2,1024,768]{2,1,0:T(8,128)(2,1)} %bitcast.145, s32[]{:T(128)S(6)} %select_n.333, s32[]{:T(128)S(6)} %select_n.330), kind=kLoop, calls=%fused_computation.7 | loop fusion | bytes 6291464 | tf_op jit(solution)/shard_map/squeeze | solution.py:149
  16.2 7.5 %convolution_multiply_fusion.refs_0_.zo_ref = f32[1024,2048]{1,0:T(8,128)} fusion(bf16[1024,768]{1,0:T(8,128)(2,1)S(1)} %copy-done, bf16[2048,768]{1,0:T(8,128)(2,1)} %to_ref.1), kind=kOutput, calls=%fused_computation.4 | convolution fusion | flops 3223322624 | bytes 13107200 | tf_op jit(solution)/shard_map/dot_general | solution.py:153
  24.3 5.8 %shard_map.67 = f32[1024,1]{1,0:T(8,128)} custom-call(f32[1024,2048]{1,0:T(8,128)} %convolution_multiply_fusion.refs_0_.zo_ref, f32[1,2048]{1,0:T(1,128)} %reshape.323.refs_1_), custom_call_target="tpu_custom_call" | custom-call | tf_op jit(solution)/shard_map/pallas_call | solution.py:40
  30.1 3.3 %collective-permute-done.1 = bf16[1024,768]{1,0:T(8,128)(2,1)} collective-permute-done((bf16[1024,768]{1,0:T(8,128)(2,1)}, bf16[1024,768]{1,0:T(8,128)(2,1)}, u32[]{:S(2)}, u32[]{:S(2)}) %collective-permute-start.1) | collective-permute-done | bytes 1572896 | tf_op jit(solution)/shard_map/ppermute | solution.py:20
  33.6 3.8 %multiply_bitcast_fusion.refs_0_.ze_ref.refs_1_ = f32[1024,1024]{1,0:T(8,128)} fusion(bf16[1024,768]{1,0:T(8,128)(2,1)S(1)} %broadcast_select_fusion.te_ref, bf16[1024,768]{1,0:T(8,128)(2,1)S(1)} %copy-done), kind=kOutput, calls=%fused_computation.5 | convolution fusion | flops 1611661312 | bytes 7340032 | tf_op jit(solution)/shard_map/dot_general | solution.py:157
  38.0 4.5 %shard_map.68 = f32[1024,1]{1,0:T(8,128)} custom-call(f32[1024,1024]{1,0:T(8,128)} %multiply_bitcast_fusion.refs_0_.ze_ref.refs_1_, f32[1,1024]{1,0:T(1,128)} %reshape.324.refs_1_), custom_call_target="tpu_custom_call" | custom-call | tf_op jit(solution)/shard_map/pallas_call | solution.py:40
  52.8 7.4 %shard_map.69 = (f32[1,2048]{1,0:T(1,128)}, f32[1,1024]{1,0:T(1,128)}) custom-call(f32[1024,2048]{1,0:T(8,128)} %convolution_multiply_fusion.refs_0_.zo_ref, f32[1024,1024]{1,0:T(8,128)} %multiply_bitcast_fusion.refs_0_.ze_ref.refs_1_, f32[1024,1]{1,0:T(8,128)} %copy.13.f_ref), custom_call_target="tpu_custom_call" | custom-call | tf_op jit(solution)/shard_map/pallas_call | solution.py:61
  60.2 4.5 %collective-permute-start.6 = (f32[1024]{0:T(1024)S(1)}, f32[1024]{0:T(1024)S(1)}, u32[]{:S(2)}, u32[]{:S(2)}) collective-permute-start(f32[1024]{0:T(1024)S(1)} %bitcast.168), channel_id=1, source_target_pairs={{0,4},{4,8},{8,12},{12,16},{16,20},{20,24},{24,28},{28,32},{32,36}... | collective-permute-start | bytes 12296 | tf_op jit(solution)/shard_map/ppermute | solution.py:20
  66.3 4.7 %collective-permute-done.5 = f32[1024]{0:T(1024)S(1)} collective-permute-done((f32[1024]{0:T(1024)S(1)}, f32[1024]{0:T(1024)S(1)}, u32[]{:S(2)}, u32[]{:S(2)}) %collective-permute-start.5) | collective-permute-done | bytes 4128 | tf_op jit(solution)/shard_map/ppermute | solution.py:20
  73.7 4.2 %collective-permute-start.7 = (f32[1024]{0:T(1024)S(1)}, f32[1024]{0:T(1024)S(1)}, u32[]{:S(2)}, u32[]{:S(2)}) collective-permute-start(f32[1024]{0:T(1024)S(1)} %bitcast.179), channel_id=1, source_target_pairs={{0,4},{4,8},{8,12},{12,16},{16,20},{20,24},{24,28},{28,32},{32,36}... | collective-permute-start | bytes 12296 | tf_op jit(solution)/shard_map/ppermute | solution.py:20
  84.9 7.1 %shard_map.70 = f32[1024,1]{1,0:T(8,128)} custom-call(f32[1024,2048]{1,0:T(8,128)} %convolution_multiply_fusion.refs_0_.zo_ref, f32[1024,1024]{1,0:T(8,128)} %multiply_bitcast_fusion.refs_0_.ze_ref.refs_1_, f32[1,2048]{1,0:T(1,128)} %get-tuple-element.35.refs_2_, f32[1,1024]{1,0:T(1,128)} %bitcast.161), custom_call_target="tpu_custom_call" | custom-call | tf_op jit(solution)/shard_map/pallas_call | solution.py:40
  100.0 7.4 %shard_map.71 = (f32[1,2048]{1,0:T(1,128)}, f32[1,1024]{1,0:T(1,128)}) custom-call(f32[1024,2048]{1,0:T(8,128)} %convolution_multiply_fusion.refs_0_.zo_ref, f32[1024,1024]{1,0:T(8,128)} %multiply_bitcast_fusion.refs_0_.ze_ref.refs_1_, f32[1024,1]{1,0:T(8,128)} %copy.14.f_ref), custom_call_target="tpu_custom_call" | custom-call | tf_op jit(solution)/shard_map/pallas_call | solution.py:61
  107.4 4.8 %collective-permute-start.15 = (f32[1024]{0:T(1024)S(1)}, f32[1024]{0:T(1024)S(1)}, u32[]{:S(2)}, u32[]{:S(2)}) collective-permute-start(f32[1024]{0:T(1024)S(1)} %bitcast.173), channel_id=1, source_target_pairs={{0,4},{4,8},{8,12},{12,16},{16,20},{20,24},{24,28},{28,32},{32,36}... | collective-permute-start | bytes 12296 | tf_op jit(solution)/shard_map/ppermute | solution.py:20
  113.7 4.8 %collective-permute-done.14 = f32[1024]{0:T(1024)S(1)} collective-permute-done((f32[1024]{0:T(1024)S(1)}, f32[1024]{0:T(1024)S(1)}, u32[]{:S(2)}, u32[]{:S(2)}) %collective-permute-start.14) | collective-permute-done | bytes 4128 | tf_op jit(solution)/shard_map/ppermute | solution.py:20
  120.6 4.2 %collective-permute-start.16 = (f32[1024]{0:T(1024)S(1)}, f32[1024]{0:T(1024)S(1)}, u32[]{:S(2)}, u32[]{:S(2)}) collective-permute-start(f32[1024]{0:T(1024)S(1)} %bitcast.181), channel_id=1, source_target_pairs={{0,4},{4,8},{8,12},{12,16},{16,20},{20,24},{24,28},{28,32},{32,36}... | collective-permute-start | bytes 12296 | tf_op jit(solution)/shard_map/ppermute | solution.py:20
  125.5 5.6 %collective-permute-done.17 = f32[1024]{0:T(1024)S(1)} collective-permute-done((f32[1024]{0:T(1024)S(1)}, f32[1024]{0:T(1024)S(1)}, u32[]{:S(2)}, u32[]{:S(2)}) %collective-permute-start.17) | collective-permute-done | bytes 4128 | tf_op jit(solution)/shard_map/ppermute | solution.py:20
  131.8 7.1 %shard_map.72 = f32[1024,1]{1,0:T(8,128)} custom-call(f32[1024,2048]{1,0:T(8,128)} %convolution_multiply_fusion.refs_0_.zo_ref, f32[1024,1024]{1,0:T(8,128)} %multiply_bitcast_fusion.refs_0_.ze_ref.refs_1_, f32[1,2048]{1,0:T(1,128)} %get-tuple-element.26.refs_2_.go_ref, f32[1,1024]{1,0:T(1,128)} %bitcast.154), custom_call_target="tpu_custom_call" | custom-call | tf_op jit(solution)/shard_map/pallas_call | solution.py:40
  147.9 11.4 %shard_map.73 = f32[1024,768]{1,0:T(8,128)} custom-call(f32[1024,2048]{1,0:T(8,128)} %convolution_multiply_fusion.refs_0_.zo_ref, f32[1024,1024]{1,0:T(8,128)} %multiply_bitcast_fusion.refs_0_.ze_ref.refs_1_, f32[1,2048]{1,0:T(1,128)} %get-tuple-element.26.refs_2_.go_ref, f32[1,1024]{1,0:T(1,128)} %bitcast.155, f32[1024,1]{1,0:T(8,128)} %copy.15.l_ref, ...), custom_call_target="tpu_custom_call" | custom-call | tf_op jit(solution)/shard_map/pallas_call | solution.py:91
  163.8 6.4 %collective-permute-done.23 = f32[128,768]{1,0:T(8,128)S(1)} collective-permute-done((f32[128,768]{1,0:T(8,128)S(1)}, f32[128,768]{1,0:T(8,128)S(1)}, u32[]{:S(2)}, u32[]{:S(2)}) %collective-permute-start.23) | collective-permute-done | bytes 393248 | tf_op jit(solution)/shard_map/ppermute | solution.py:20
  171.4 3.0 %collective-permute-start.26 = (f32[2,128,768]{2,1,0:T(8,128)S(1)}, f32[2,128,768]{2,1,0:T(8,128)S(1)}, u32[]{:S(2)}, u32[]{:S(2)}) collective-permute-start(f32[2,128,768]{2,1,0:T(8,128)S(1)} %pad_maximum_fusion.2), channel_id=1, source_target_pairs={{0,3},{1,0},{2,1},{3,2},{4,7},{5,4},{6,5},{7,6},{8,11},{9,8},{10,9... | collective-permute-start | bytes 2359304 | tf_op jit(solution)/shard_map/ppermute | solution.py:20
  174.6 15.7 %collective-permute-done.26 = f32[2,128,768]{2,1,0:T(8,128)S(1)} collective-permute-done((f32[2,128,768]{2,1,0:T(8,128)S(1)}, f32[2,128,768]{2,1,0:T(8,128)S(1)}, u32[]{:S(2)}, u32[]{:S(2)}) %collective-permute-start.26) | collective-permute-done | bytes 786464 | tf_op jit(solution)/shard_map/ppermute | solution.py:20
  190.2 3.5 %collective-permute-done.24 = f32[2,128,768]{2,1,0:T(8,128)S(1)} collective-permute-done((f32[2,128,768]{2,1,0:T(8,128)S(1)}, f32[2,128,768]{2,1,0:T(8,128)S(1)}, u32[]{:S(2)}, u32[]{:S(2)}) %collective-permute-start.24) | collective-permute-done | bytes 786464 | tf_op jit(solution)/shard_map/ppermute | solution.py:20
  195.5 9.5 %collective-permute-done.29 = bf16[256,768]{1,0:T(8,128)(2,1)S(1)} collective-permute-done((bf16[256,768]{1,0:T(8,128)(2,1)S(1)}, bf16[256,768]{1,0:T(8,128)(2,1)S(1)}, u32[]{:S(2)}, u32[]{:S(2)}) %collective-permute-start.29) | collective-permute-done | bytes 393248 | tf_op jit(solution)/shard_map/ppermute | solution.py:20
  207.3 4.0 %collective-permute-done.30 = bf16[128,768]{1,0:T(8,128)(2,1)S(1)} collective-permute-done((bf16[128,768]{1,0:T(8,128)(2,1)S(1)}, bf16[128,768]{1,0:T(8,128)(2,1)S(1)}, u32[]{:S(2)}, u32[]{:S(2)}) %collective-permute-start.30) | collective-permute-done | bytes 196640 | tf_op jit(solution)/shard_map/ppermute | solution.py:20
  (118 shorter events, 56.6 us)
Async XLA Ops:
  9.9 20.2 %collective-permute-start = (bf16[1024,768]{1,0:T(8,128)(2,1)}, bf16[1024,768]{1,0:T(8,128)(2,1)S(1)}, u32[]{:S(2)}, u32[]{:S(2)}) collective-permute-start(bf16[1024,768]{1,0:T(8,128)(2,1)} %get-tuple-element.22), channel_id=1, source_target_pairs={{0,4},{4,8},{8,12},{12,16},{16,20},{20,24},{24,28},{28,32},{32,36}... | collective-permute-start | bytes 4718600 | tf_op jit(solution)/shard_map/ppermute | solution.py:20
  9.9 23.5 %collective-permute-start.1 = (bf16[1024,768]{1,0:T(8,128)(2,1)}, bf16[1024,768]{1,0:T(8,128)(2,1)}, u32[]{:S(2)}, u32[]{:S(2)}) collective-permute-start(bf16[1024,768]{1,0:T(8,128)(2,1)} %get-tuple-element.21), channel_id=1, source_target_pairs={{0,124},{4,0},{8,4},{12,8},{16,12},{20,16},{24,20},{28,24},{32,28}... | collective-permute-start | bytes 4718600 | tf_op jit(solution)/shard_map/ppermute | solution.py:20
  44.0 5.0 %collective-permute-start.4 = (f32[1024]{0:T(1024)S(1)}, f32[1024]{0:T(1024)S(1)}, u32[]{:S(2)}, u32[]{:S(2)}) collective-permute-start(f32[1024]{0:T(1024)S(1)} %select_reduce_fusion), channel_id=1, source_target_pairs={{0,3},{1,0},{2,1},{3,2},{4,7},{5,4},{6,5},{7,6},{8,11},{9,8},{10,9... | collective-permute-start | bytes 12296 | tf_op jit(solution)/shard_map/ppermute | solution.py:20
  60.2 6.1 %collective-permute-start.6 = (f32[1024]{0:T(1024)S(1)}, f32[1024]{0:T(1024)S(1)}, u32[]{:S(2)}, u32[]{:S(2)}) collective-permute-start(f32[1024]{0:T(1024)S(1)} %bitcast.168), channel_id=1, source_target_pairs={{0,4},{4,8},{8,12},{12,16},{16,20},{20,24},{24,28},{28,32},{32,36}... | collective-permute-start | bytes 12296 | tf_op jit(solution)/shard_map/ppermute | solution.py:20
  64.7 6.4 %collective-permute-start.5 = (f32[1024]{0:T(1024)S(1)}, f32[1024]{0:T(1024)S(1)}, u32[]{:S(2)}, u32[]{:S(2)}) collective-permute-start(f32[1024]{0:T(1024)S(1)} %bitcast.169), channel_id=1, source_target_pairs={{0,124},{4,0},{8,4},{12,8},{16,12},{20,16},{24,20},{28,24},{32,28}... | collective-permute-start | bytes 12296 | tf_op jit(solution)/shard_map/ppermute | solution.py:20
  64.7 17.1 %collective-permute-start.9 = (f32[1024]{0:T(1024)S(1)}, f32[1024]{0:T(1024)S(1)}, u32[]{:S(2)}, u32[]{:S(2)}) collective-permute-start(f32[1024]{0:T(1024)S(1)} %bitcast.170), channel_id=1, source_target_pairs={{0,8},{4,12},{8,16},{12,20},{16,24},{20,28},{24,32},{28,36},{32,40... | collective-permute-start | bytes 12296 | tf_op jit(solution)/shard_map/ppermute | solution.py:20
  64.9 17.0 %collective-permute-start.10 = (f32[1024]{0:T(1024)S(1)}, f32[1024]{0:T(1024)S(1)}, u32[]{:S(2)}, u32[]{:S(2)}) collective-permute-start(f32[1024]{0:T(1024)S(1)} %bitcast.171), channel_id=1, source_target_pairs={{0,120},{4,124},{8,0},{12,4},{16,8},{20,12},{24,16},{28,20},{32,24... | collective-permute-start | bytes 12296 | tf_op jit(solution)/shard_map/ppermute | solution.py:20
  73.7 8.2 %collective-permute-start.7 = (f32[1024]{0:T(1024)S(1)}, f32[1024]{0:T(1024)S(1)}, u32[]{:S(2)}, u32[]{:S(2)}) collective-permute-start(f32[1024]{0:T(1024)S(1)} %bitcast.179), channel_id=1, source_target_pairs={{0,4},{4,8},{8,12},{12,16},{16,20},{20,24},{24,28},{28,32},{32,36}... | collective-permute-start | bytes 12296 | tf_op jit(solution)/shard_map/ppermute | solution.py:20
  78.0 6.4 %collective-permute-start.8 = (f32[1024]{0:T(1024)S(1)}, f32[1024]{0:T(1024)S(1)}, u32[]{:S(2)}, u32[]{:S(2)}) collective-permute-start(f32[1024]{0:T(1024)S(1)} %bitcast.178), channel_id=1, source_target_pairs={{0,124},{4,0},{8,4},{12,8},{16,12},{20,16},{24,20},{28,24},{32,28}... | collective-permute-start | bytes 12296 | tf_op jit(solution)/shard_map/ppermute | solution.py:20
  93.5 4.7 %collective-permute-start.11 = (f32[1024]{0:T(1024)S(1)}, f32[1024]{0:T(1024)S(1)}, u32[]{:S(2)}, u32[]{:S(2)}) collective-permute-start(f32[1024]{0:T(1024)S(1)} %reduce.6), channel_id=1, source_target_pairs={{0,1},{1,2},{2,3},{3,0},{4,5},{5,6},{6,7},{7,4},{8,9},{9,10},{10,1... | collective-permute-start | bytes 12296 | tf_op jit(solution)/shard_map/ppermute | solution.py:20
  107.4 6.2 %collective-permute-start.15 = (f32[1024]{0:T(1024)S(1)}, f32[1024]{0:T(1024)S(1)}, u32[]{:S(2)}, u32[]{:S(2)}) collective-permute-start(f32[1024]{0:T(1024)S(1)} %bitcast.173), channel_id=1, source_target_pairs={{0,4},{4,8},{8,12},{12,16},{16,20},{20,24},{24,28},{28,32},{32,36}... | collective-permute-start | bytes 12296 | tf_op jit(solution)/shard_map/ppermute | solution.py:20
  112.1 6.4 %collective-permute-start.14 = (f32[1024]{0:T(1024)S(1)}, f32[1024]{0:T(1024)S(1)}, u32[]{:S(2)}, u32[]{:S(2)}) collective-permute-start(f32[1024]{0:T(1024)S(1)} %bitcast.174), channel_id=1, source_target_pairs={{0,124},{4,0},{8,4},{12,8},{16,12},{20,16},{24,20},{28,24},{32,28}... | collective-permute-start | bytes 12296 | tf_op jit(solution)/shard_map/ppermute | solution.py:20
  112.1 12.7 %collective-permute-start.18 = (f32[1024]{0:T(1024)S(1)}, f32[1024]{0:T(1024)S(1)}, u32[]{:S(2)}, u32[]{:S(2)}) collective-permute-start(f32[1024]{0:T(1024)S(1)} %bitcast.175), channel_id=1, source_target_pairs={{0,8},{4,12},{8,16},{12,20},{16,24},{20,28},{24,32},{28,36},{32,40... | collective-permute-start | bytes 12296 | tf_op jit(solution)/shard_map/ppermute | solution.py:20
  112.3 12.5 %collective-permute-start.19 = (f32[1024]{0:T(1024)S(1)}, f32[1024]{0:T(1024)S(1)}, u32[]{:S(2)}, u32[]{:S(2)}) collective-permute-start(f32[1024]{0:T(1024)S(1)} %bitcast.176), channel_id=1, source_target_pairs={{0,120},{4,124},{8,0},{12,4},{16,8},{20,12},{24,16},{28,20},{32,24... | collective-permute-start | bytes 12296 | tf_op jit(solution)/shard_map/ppermute | solution.py:20
  120.6 5.0 %collective-permute-start.16 = (f32[1024]{0:T(1024)S(1)}, f32[1024]{0:T(1024)S(1)}, u32[]{:S(2)}, u32[]{:S(2)}) collective-permute-start(f32[1024]{0:T(1024)S(1)} %bitcast.181), channel_id=1, source_target_pairs={{0,4},{4,8},{8,12},{12,16},{16,20},{20,24},{24,28},{28,32},{32,36}... | collective-permute-start | bytes 12296 | tf_op jit(solution)/shard_map/ppermute | solution.py:20
  124.8 6.4 %collective-permute-start.17 = (f32[1024]{0:T(1024)S(1)}, f32[1024]{0:T(1024)S(1)}, u32[]{:S(2)}, u32[]{:S(2)}) collective-permute-start(f32[1024]{0:T(1024)S(1)} %bitcast.180), channel_id=1, source_target_pairs={{0,124},{4,0},{8,4},{12,8},{16,12},{20,16},{24,20},{28,24},{32,28}... | collective-permute-start | bytes 12296 | tf_op jit(solution)/shard_map/ppermute | solution.py:20
  161.0 9.1 %collective-permute-start.23 = (f32[128,768]{1,0:T(8,128)S(1)}, f32[128,768]{1,0:T(8,128)S(1)}, u32[]{:S(2)}, u32[]{:S(2)}) collective-permute-start(f32[128,768]{1,0:T(8,128)S(1)} %get-tuple-element.15), channel_id=1, source_target_pairs={{0,1},{1,2},{2,3},{3,0},{4,5},{5,6},{6,7},{7,4},{8,9},{9,10},{10,1... | collective-permute-start | bytes 1179656 | tf_op jit(solution)/shard_map/ppermute | solution.py:20
  161.1 9.0 %collective-permute-start.25 = (f32[128,768]{1,0:T(8,128)S(1)}, f32[128,768]{1,0:T(8,128)S(1)}, u32[]{:S(2)}, u32[]{:S(2)}) collective-permute-start(f32[128,768]{1,0:T(8,128)S(1)} %get-tuple-element.16), channel_id=1, source_target_pairs={{0,3},{1,0},{2,1},{3,2},{4,7},{5,4},{6,5},{7,6},{8,11},{9,8},{10,9... | collective-permute-start | bytes 1179656 | tf_op jit(solution)/shard_map/ppermute | solution.py:20
  171.4 18.8 %collective-permute-start.26 = (f32[2,128,768]{2,1,0:T(8,128)S(1)}, f32[2,128,768]{2,1,0:T(8,128)S(1)}, u32[]{:S(2)}, u32[]{:S(2)}) collective-permute-start(f32[2,128,768]{2,1,0:T(8,128)S(1)} %pad_maximum_fusion.2), channel_id=1, source_target_pairs={{0,3},{1,0},{2,1},{3,2},{4,7},{5,4},{6,5},{7,6},{8,11},{9,8},{10,9... | collective-permute-start | bytes 2359304 | tf_op jit(solution)/shard_map/ppermute | solution.py:20
  174.5 19.3 %collective-permute-start.24 = (f32[2,128,768]{2,1,0:T(8,128)S(1)}, f32[2,128,768]{2,1,0:T(8,128)S(1)}, u32[]{:S(2)}, u32[]{:S(2)}) collective-permute-start(f32[2,128,768]{2,1,0:T(8,128)S(1)} %pad_maximum_fusion.1), channel_id=1, source_target_pairs={{0,1},{1,2},{2,3},{3,0},{4,5},{5,6},{6,7},{7,4},{8,9},{9,10},{10,1... | collective-permute-start | bytes 2359304 | tf_op jit(solution)/shard_map/ppermute | solution.py:20
  193.9 11.1 %collective-permute-start.29 = (bf16[256,768]{1,0:T(8,128)(2,1)S(1)}, bf16[256,768]{1,0:T(8,128)(2,1)S(1)}, u32[]{:S(2)}, u32[]{:S(2)}) collective-permute-start(bf16[256,768]{1,0:T(8,128)(2,1)S(1)} %bitcast.149), channel_id=1, source_target_pairs={{0,3},{1,0},{2,1},{3,2},{4,7},{5,4},{6,5},{7,6},{8,11},{9,8},{10,9... | collective-permute-start | bytes 1179656 | tf_op jit(solution)/shard_map/ppermute | solution.py:20
  194.0 12.1 %collective-permute-start.27 = (bf16[256,768]{1,0:T(8,128)(2,1)S(1)}, bf16[256,768]{1,0:T(8,128)(2,1)S(1)}, u32[]{:S(2)}, u32[]{:S(2)}) collective-permute-start(bf16[256,768]{1,0:T(8,128)(2,1)S(1)} %bitcast.150), channel_id=1, source_target_pairs={{0,1},{1,2},{2,3},{3,0},{4,5},{5,6},{6,7},{7,4},{8,9},{9,10},{10,1... | collective-permute-start | bytes 1179656 | tf_op jit(solution)/shard_map/ppermute | solution.py:20
  205.0 6.3 %collective-permute-start.30 = (bf16[128,768]{1,0:T(8,128)(2,1)S(1)}, bf16[128,768]{1,0:T(8,128)(2,1)S(1)}, u32[]{:S(2)}, u32[]{:S(2)}) collective-permute-start(bf16[128,768]{1,0:T(8,128)(2,1)S(1)} %slice.69), channel_id=1, source_target_pairs={{0,3},{1,0},{2,1},{3,2},{4,7},{5,4},{6,5},{7,6},{8,11},{9,8},{10,9... | collective-permute-start | bytes 589832 | tf_op jit(solution)/shard_map/ppermute | solution.py:20
  206.2 7.3 %collective-permute-start.28 = (bf16[128,768]{1,0:T(8,128)(2,1)S(1)}, bf16[128,768]{1,0:T(8,128)(2,1)S(1)}, u32[]{:S(2)}, u32[]{:S(2)}) collective-permute-start(bf16[128,768]{1,0:T(8,128)(2,1)S(1)} %slice.68), channel_id=1, source_target_pairs={{0,1},{1,2},{2,3},{3,0},{4,5},{5,6},{6,7},{7,4},{8,9},{9,10},{10,1... | collective-permute-start | bytes 589832 | tf_op jit(solution)/shard_map/ppermute | solution.py:20
  (12 other events, 69.4 us)
